TPU v7x, 128 devices: a whole 4x4x4 slice. The times are simulated.
128 devices in a mesh: batch: 4 (over y), region: 32 (over x, z, core).
Axes of the slice: x: 4, y: 4, z: 4, core: 2. Of those that a mesh axis runs over, the one named last changes fastest.
Arguments:
- leaves: float32 [256, 4096, 256], P('region', 'batch'), may hold values from -66 to 66
- leaf_order: int32 [32, 8], replicated, may hold values from 0 to 7, each once within a row
- node_order: int32 [32, 4], replicated, may hold values from 0 to 3, each once within a row
- weight_one: float32 [128, 256, 256], P('region'), may hold values from 0.001 to 0.04
- weight_two: float32 [64, 256, 256], P('region'), may hold values from 0.001 to 0.04
- top_adjoint: float32 [64, 4096, 256], P('region', 'batch'), may hold values from -6 to 6
Outputs:
- top_log: float32 [64, 4096, 256], P('region', 'batch')
- leaf_adjoint: float32 [256, 4096, 256], P('region', 'batch')
- grad_one: float32 [128, 256, 256], P('region')
- grad_two: float32 [64, 256, 256], P('region')
Inputs may be any that keep to these rules, and one draw needn't show every extreme that they name: Each row of leaf_order is a permutation of 0 to 7. Each row of node_order is a permutation of 0 to 3.
All inputs are finite; a program needn't handle non-finite values.
Results may differ from a plain program's by a relative error of at most 0.0003.
Values sent between devices are 32-bit elements; how exact they have to be, the bound alone decides.
No kernel may reach another device: no remote copies, remote signals or barrier semaphores. Data moves between devices by JAX's collectives and lax.ppermute only.
A program may use at most 128 MiB of HBM per device.

v0:
```python
import jax
import jax.numpy as jnp
from jax import lax
from jax.sharding import PartitionSpec as P


def from_partner(value, axis, distance):
    mask = 2**distance
    pairs = [(source, source ^ mask) for source in range(lax.axis_size(axis))]
    return lax.ppermute(value, axis, pairs)


def mixture(left, right, weight):
    summed = left + right
    peak = jnp.max(summed, axis=2, keepdims=True)
    scaled = jnp.exp(summed - peak)
    totals = jnp.einsum("nbi,noi->nbo", scaled, weight, precision=lax.Precision.HIGHEST)
    return (peak + jnp.log(totals), scaled, totals)


def descend(adjoint, scaled, totals, weight):
    ratio = adjoint / totals
    counts = jnp.einsum("nbo,nbi->noi", ratio, scaled, precision=lax.Precision.HIGHEST)
    spread = scaled * jnp.einsum("nbo,noi->nbi", ratio, weight, precision=lax.Precision.HIGHEST)
    return (counts, spread)


def local(leaves, leaf_order, node_order, weight_one, weight_two, top_adjoint):
    here = lax.axis_index("region")
    across = jnp.bitwise_xor(here, jnp.int32(1))
    beyond = jnp.bitwise_xor(here, jnp.int32(2))
    first = weight_one.shape[0]
    second = weight_two.shape[0]
    own_leaf = lax.dynamic_index_in_dim(leaf_order, here, 0, keepdims=False)
    other_leaf = lax.dynamic_index_in_dim(leaf_order, across, 0, keepdims=False)
    own_node = lax.dynamic_index_in_dim(node_order, here, 0, keepdims=False)
    other_node = lax.dynamic_index_in_dim(node_order, beyond, 0, keepdims=False)
    left_one = jnp.take(leaves, own_leaf[:first], axis=0)
    partner_leaves = from_partner(leaves, "region", 0)
    right_one = jnp.take(partner_leaves, other_leaf[first:], axis=0)
    level_one, scaled_one, totals_one = mixture(left_one, right_one, weight_one)
    left_two = jnp.take(level_one, own_node[:second], axis=0)
    partner_nodes = from_partner(level_one, "region", 1)
    right_two = jnp.take(partner_nodes, other_node[second:], axis=0)
    top_log, scaled_two, totals_two = mixture(left_two, right_two, weight_two)
    counts_two, spread_two = descend(top_adjoint, scaled_two, totals_two, weight_two)
    returned_two = from_partner(spread_two, "region", 1)
    placed_two = jnp.concatenate([spread_two, returned_two], axis=0)
    adjoint_one = jnp.take(placed_two, jnp.argsort(own_node), axis=0)
    counts_one, spread_one = descend(adjoint_one, scaled_one, totals_one, weight_one)
    grad_one, grad_two = lax.psum((counts_one, counts_two), "batch")
    returned_one = from_partner(spread_one, "region", 0)
    placed_one = jnp.concatenate([spread_one, returned_one], axis=0)
    leaf_adjoint = jnp.take(placed_one, jnp.argsort(own_leaf), axis=0)
    return (top_log, leaf_adjoint, grad_one, grad_two)


def solution(mesh):
    return jax.shard_map(
        local,
        mesh=mesh,
        in_specs=(
            P("region", "batch", None),
            P(),
            P(),
            P("region", None, None),
            P("region", None, None),
            P("region", "batch", None),
        ),
        out_specs=(
            P("region", "batch", None),
            P("region", "batch", None),
            P("region", None, None),
            P("region", None, None),
        ),
        check_vma=False,
    )
```

profile of v0, /device:TPU:1, one launch (start us, length us, event | category | flops | bytes accessed | tf_op | source)
XLA Modules:
  0.0 290.4 jit_solution(1506756985983288583)
XLA Ops:
  7.2 0.0 copy-start
  7.2 0.0 all-reduce.3.cloned.1.call-start
  7.2 1.5 collective-permute-start
  8.7 0.9 fusion.11
  9.6 0.1 slice_reduce_fusion.1
  9.8 6.2 %gather_fusion.2 = f32[4,1024,256]{2,1,0:T(8,128)} fusion(f32[8,1024,256]{2,1,0:T(8,128)} %param.10, s32[1024]{0:T(1024)S(1)} %pad_clamp_fusion.5), kind=kCustom, calls=%fused_computation.clone | custom fusion | bytes 8388624 | tf_op jit(solution)/shard_map/jit(_take)/gather | solution.py:38
  15.9 0.1 slice_reduce_fusion
  16.1 5.7 %collective-permute-done = f32[8,1024,256]{2,1,0:T(8,128)} collective-permute-done((f32[8,1024,256]{2,1,0:T(8,128)}, f32[8,1024,256]{2,1,0:T(8,128)}, u32[]{:S(2)}, u32[]{:S(2)}) %collective-permute-start) | collective-permute-done | bytes 8388640 | tf_op jit(solution)/shard_map/ppermute | solution.py:10
  21.8 6.2 %gather_fusion.3 = f32[4,1024,256]{2,1,0:T(8,128)} fusion(f32[8,1024,256]{2,1,0:T(8,128)} %collective-permute-done, s32[1024]{0:T(1024)S(1)} %pad_clamp_fusion.4), kind=kCustom, calls=%fused_computation.2.clone | custom fusion | bytes 8388624 | tf_op jit(solution)/shard_map/jit(_take)/gather | solution.py:40
  28.0 4.2 %fusion.14 = (f32[4,1024]{1,0:T(4,128)S(1)}, f32[4,1024,256]{2,1,0:T(8,128)S(1)}) fusion(f32[4,1024,256]{2,1,0:T(8,128)} %gather_fusion.3, pred[4]{0:T(512)(128)(4,1)S(1)} %get-tuple-element.28, f32[4,1024,256]{2,1,0:T(8,128)} %gather_fusion.2, pred[4]{0:T(512)(128)(4,1)S(1)} %get-tuple-element.29), kind=kLoop, calls=%fused_computation.57 | loop fusion | flops 4190208 | bytes 12599304 | tf_op jit(solution)/shard_map/reduce_max | solution.py:15
  32.2 0.0 copy-done
  32.2 0.0 copy-start.9
  32.2 6.9 %log_add_fusion = (f32[4,1024,256]{2,1,0:T(8,128)}, f32[4,1024,256]{2,1,0:T(8,128)}) fusion(f32[4,1024]{1,0:T(4,128)S(1)} %get-tuple-element.18, f32[4,256,256]{2,1,0:T(8,128)S(1)} %copy-done, f32[4,1024,256]{2,1,0:T(8,128)S(1)} %get-tuple-element.19), kind=kOutput, calls=%fused_computation.11 | convolution fusion | flops 3223322624 | bytes 13647872 | tf_op jit(solution)/shard_map/nbi,noi->nbo/dot_general | solution.py:17
  39.1 0.0 copy-done.2
  39.1 1.7 collective-permute-start.1
  40.8 0.0 copy-done.9
  40.9 0.2 fusion.12
  41.0 0.1 slice_reduce_fusion.3
  41.2 0.1 slice_reduce_fusion.2
  41.3 2.9 gather_fusion.4
  44.2 87.5 %collective-permute-done.1 = f32[4,1024,256]{2,1,0:T(8,128)} collective-permute-done((f32[4,1024,256]{2,1,0:T(8,128)}, f32[4,1024,256]{2,1,0:T(8,128)}, u32[]{:S(2)}, u32[]{:S(2)}) %collective-permute-start.1) | collective-permute-done | bytes 4194336 | tf_op jit(solution)/shard_map/ppermute | solution.py:10
  131.7 4.2 %gather_fusion.5 = f32[2,1024,256]{2,1,0:T(8,128)} fusion(f32[4,1024,256]{2,1,0:T(8,128)} %collective-permute-done.1, s32[1024]{0:T(1024)S(1)} %pad_clamp_fusion.2), kind=kCustom, calls=%fused_computation.3.clone | custom fusion | bytes 4194312 | tf_op jit(solution)/shard_map/jit(_take)/gather | solution.py:44
  135.9 2.1 fusion.13
  138.0 0.0 copy-start.4
  138.0 0.0 copy-start.10
  138.0 0.0 copy-done.8
  138.0 3.1 %log_add_fusion.1 = (f32[2,1024,256]{2,1,0:T(8,128)}, f32[2,1024,256]{2,1,0:T(8,128)S(1)}) fusion(f32[2,1024]{1,0:T(2,128)S(1)} %get-tuple-element.16, f32[2,256,256]{2,1,0:T(8,128)S(1)} %copy-done.8, f32[2,1024,256]{2,1,0:T(8,128)S(1)} %get-tuple-element.17), kind=kOutput, calls=%fused_computation.17 | convolution fusion | flops 1611661312 | bytes 6823936 | tf_op jit(solution)/shard_map/nbi,noi->nbo/dot_general | solution.py:17
  141.2 3.6 %convolution_multiply_fusion = f32[2,1024,256]{2,1,0:T(8,128)} fusion(f32[2,256,256]{2,1,0:T(8,128)S(1)} %copy-done.8, f32[2,1024,256]{2,1,0:T(8,128)S(1)} %get-tuple-element.17, f32[2,1024]{1,0:T(2,128)S(1)} %get-tuple-element.16, f32[2,1024,256]{2,1,0:T(8,128)S(1)} %copy-done.10, f32[2,1024,256]{2,1,0:T(8,128)S(1)} %get-tuple-element.25), kind=kOutput, calls=%fused_computation.21 | convolution fusion | flops 1612185600 | bytes 8921088 | tf_op jit(solution)/shard_map/nbo,noi->nbi/dot_general | solution.py:24
  144.8 0.0 copy-done.4
  144.8 1.2 collective-permute-start.2
  146.0 0.7 sort.35
  146.8 44.6 %collective-permute-done.2 = f32[2,1024,256]{2,1,0:T(8,128)} collective-permute-done((f32[2,1024,256]{2,1,0:T(8,128)}, f32[2,1024,256]{2,1,0:T(8,128)}, u32[]{:S(2)}, u32[]{:S(2)}) %collective-permute-start.2) | collective-permute-done | bytes 2097184 | tf_op jit(solution)/shard_map/ppermute | solution.py:10
  191.3 4.6 %pad_maximum_fusion.1 = f32[4,1024,256]{2,1,0:T(8,128)} fusion(f32[2,1024,256]{2,1,0:T(8,128)} %collective-permute-done.2, f32[2,1024,256]{2,1,0:T(8,128)} %convolution_multiply_fusion), kind=kLoop, calls=%fused_computation.7 | loop fusion | flops 1048576 | bytes 8388608 | tf_op jit(solution)/shard_map/concatenate | solution.py:48
  195.9 4.9 %gather_fusion = f32[4,1024,256]{2,1,0:T(8,128)} fusion(f32[4,1024,256]{2,1,0:T(8,128)} %pad_maximum_fusion.1, s32[1024]{0:T(1024)S(1)} %pad_clamp_fusion.1), kind=kCustom, calls=%fused_computation.4 | custom fusion | bytes 8388624 | tf_op jit(solution)/shard_map/jit(_take)/gather | solution.py:49
  200.9 11.3 %fusion.1 = f32[4,1024,256]{2,1,0:T(8,128)} fusion(f32[4,1024,256]{2,1,0:T(8,128)} %copy-done.2, f32[4,256,256]{2,1,0:T(8,128)S(1)} %copy-done, f32[4,1024]{1,0:T(4,128)S(1)} %get-tuple-element.18, f32[4,1024,256]{2,1,0:T(8,128)} %get-tuple-element.23, f32[4,1024,256]{2,1,0:T(8,128)} %gather_fusion, pred[4]{0:T(512)(128)(4,1)S(1)} %compare_and_fusion.4), kind=kOutput, calls=%fused_computation.14 | convolution fusion | flops 3225419776 | bytes 17842180 | tf_op jit(solution)/shard_map/nbo,noi->nbi/dot_general | solution.py:24
  212.2 1.8 collective-permute-start.3
  214.0 0.0 copy-done.5
  214.0 4.7 %fusion.5 = f32[2,256,256]{2,1,0:T(8,128)} fusion(f32[2,1024,256]{2,1,0:T(8,128)S(1)} %copy-done.5, f32[2,1024]{1,0:T(2,128)S(1)} %get-tuple-element.16, f32[2,1024,256]{2,1,0:T(8,128)S(1)} %copy-done.11, f32[2,1024,256]{2,1,0:T(8,128)S(1)} %get-tuple-element.25), kind=kOutput, calls=%fused_computation.22 | convolution fusion | flops 1611661312 | bytes 6823936 | tf_op jit(solution)/shard_map/nbo,nbi->noi/dot_general | solution.py:23
  218.8 8.7 %fusion = f32[4,256,256]{2,1,0:T(8,128)} fusion(f32[4,1024,256]{2,1,0:T(8,128)S(1)} %copy-done.3, f32[4,1024]{1,0:T(4,128)S(1)} %get-tuple-element.18, f32[4,1024,256]{2,1,0:T(8,128)S(1)} %copy-done.7, f32[4,1024,256]{2,1,0:T(8,128)S(1)} %copy-done.6, pred[4]{0:T(512)(128)(4,1)S(1)} %compare_and_fusion.4), kind=kOutput, calls=%fused_computation.13 | convolution fusion | flops 3224371200 | bytes 13647876 | tf_op jit(solution)/shard_map/nbo,nbi->noi/dot_general | solution.py:23
  227.4 0.0 all-reduce.3.cloned.1.call-update
  227.5 1.0 sort.34
  228.5 0.0 collective-permute-done.3
  228.5 7.4 %pad_maximum_fusion = f32[8,1024,256]{2,1,0:T(8,128)} fusion(f32[4,1024,256]{2,1,0:T(8,128)} %collective-permute-done.3, f32[4,1024,256]{2,1,0:T(8,128)} %fusion.1), kind=kLoop, calls=%fused_computation.6 | loop fusion | flops 2097152 | bytes 16777216 | tf_op jit(solution)/shard_map/concatenate | solution.py:53
  235.9 8.0 %gather_fusion.1 = f32[8,1024,256]{2,1,0:T(8,128)} fusion(f32[8,1024,256]{2,1,0:T(8,128)} %pad_maximum_fusion, s32[1024]{0:T(1024)S(1)} %pad_clamp_fusion), kind=kCustom, calls=%fused_computation.5 | custom fusion | bytes 16777248 | tf_op jit(solution)/shard_map/jit(_take)/gather | solution.py:54
  243.9 8.0 %broadcast_select_fusion = f32[8,1024,256]{2,1,0:T(8,128)} fusion(f32[8,1024,256]{2,1,0:T(8,128)} %gather_fusion.1, pred[8]{0:T(512)(128)(4,1)S(1)} %compare_and_fusion.5), kind=kLoop, calls=%fused_computation.9 | loop fusion | flops 2097152 | bytes 16777224 | tf_op jit(solution)/shard_map/jit(_take)/select_n | solution.py:54
  251.8 27.6 %all-reduce.3.cloned.1.call-done = (f32[4,256,256]{2,1,0:T(8,128)}, f32[2,256,256]{2,1,0:T(8,128)}) async-done(((f32[4,256,256]{2,1,0:T(8,128)}, f32[2,256,256]{2,1,0:T(8,128)}), (f32[4,256,256]{2,1,0:T(8,128)}, f32[2,256,256]{2,1,0:T(8,128)})) %all-reduce.3.cloned.1.call-update) | async-done | bytes 1572880 | tf_op jit(solution)/shard_map/psum | solution.py:51
  279.4 2.3 copy.16
  281.7 1.9 copy.17
  (32 shorter events, 0.1 us)
Async XLA Ops:
  7.2 25.0 %copy-start = (f32[4,256,256]{2,1,0:T(8,128)S(1)}, f32[4,256,256]{2,1,0:T(8,128)}, u32[]{:S(2)}) copy-start(f32[4,256,256]{2,1,0:T(8,128)} %param.13) | copy-start | bytes 3145732
  7.2 272.3 %all-reduce.3.cloned.1.call-start = ((), (), s32[]{:S(2)}) async-start(), calls=%async_computation | async-start | bytes 3145728 | tf_op jit(solution)/shard_map/psum | solution.py:51
  7.2 14.6 %collective-permute-start = (f32[8,1024,256]{2,1,0:T(8,128)}, f32[8,1024,256]{2,1,0:T(8,128)}, u32[]{:S(2)}, u32[]{:S(2)}) collective-permute-start(f32[8,1024,256]{2,1,0:T(8,128)} %param.10), channel_id=1, source_target_pairs={{0,1},{1,0},{2,3},{3,2},{4,5},{5,4},{6,7},{7,6},{8,9},{9,8},{10,11... | collective-permute-start | bytes 25165832 | tf_op jit(solution)/shard_map/ppermute | solution.py:10
  32.2 6.9 %copy-start.2 = (f32[4,1024,256]{2,1,0:T(8,128)}, f32[4,1024,256]{2,1,0:T(8,128)S(1)}, u32[]{:S(2)}) copy-start(f32[4,1024,256]{2,1,0:T(8,128)S(1)} %get-tuple-element.19) | copy-start | bytes 12582916
  32.2 8.6 %copy-start.9 = (s32[32,4]{0,1:T(4,128)S(1)}, s32[32,4]{0,1:T(4,128)}, u32[]{:S(2)}) copy-start(s32[32,4]{0,1:T(4,128)} %param.12) | copy-start | bytes 1540
  39.1 92.6 %collective-permute-start.1 = (f32[4,1024,256]{2,1,0:T(8,128)}, f32[4,1024,256]{2,1,0:T(8,128)}, u32[]{:S(2)}, u32[]{:S(2)}) collective-permute-start(f32[4,1024,256]{2,1,0:T(8,128)} %get-tuple-element.22), channel_id=1, source_target_pairs={{0,2},{1,3},{2,0},{3,1},{4,6},{5,7},{6,4},{7,5},{8,10},{9,11},{10,... | collective-permute-start | bytes 12582920 | tf_op jit(solution)/shard_map/ppermute | solution.py:10
  135.9 2.1 copy-start.8
  138.0 6.8 %copy-start.4 = (f32[2,1024,256]{2,1,0:T(8,128)}, f32[2,1024,256]{2,1,0:T(8,128)S(1)}, u32[]{:S(2)}) copy-start(f32[2,1024,256]{2,1,0:T(8,128)S(1)} %get-tuple-element.17) | copy-start | bytes 6291460
  138.0 3.1 %copy-start.10 = (f32[2,1024,256]{2,1,0:T(8,128)S(1)}, f32[2,1024,256]{2,1,0:T(8,128)}, u32[]{:S(2)}) copy-start(f32[2,1024,256]{2,1,0:T(8,128)} %param.15) | copy-start | bytes 6291460
  144.8 46.6 %collective-permute-start.2 = (f32[2,1024,256]{2,1,0:T(8,128)}, f32[2,1024,256]{2,1,0:T(8,128)}, u32[]{:S(2)}, u32[]{:S(2)}) collective-permute-start(f32[2,1024,256]{2,1,0:T(8,128)} %convolution_multiply_fusion), channel_id=1, source_target_pairs={{0,2},{1,3},{2,0},{3,1},{4,6},{5,7},{6,4},{7,5},{8,10},{9,11},{10,... | collective-permute-start | bytes 6291464 | tf_op jit(solution)/shard_map/ppermute | solution.py:10
  200.9 13.1 %copy-start.5 = (f32[2,1024,256]{2,1,0:T(8,128)S(1)}, f32[2,1024,256]{2,1,0:T(8,128)}, u32[]{:S(2)}) copy-start(f32[2,1024,256]{2,1,0:T(8,128)} %copy-done.4) | copy-start | bytes 6291460
  200.9 13.1 %copy-start.11 = (f32[2,1024,256]{2,1,0:T(8,128)S(1)}, f32[2,1024,256]{2,1,0:T(8,128)}, u32[]{:S(2)}) copy-start(f32[2,1024,256]{2,1,0:T(8,128)} %param.15) | copy-start | bytes 6291460
  200.9 17.9 %copy-start.7 = (f32[4,1024,256]{2,1,0:T(8,128)S(1)}, f32[4,1024,256]{2,1,0:T(8,128)}, u32[]{:S(2)}) copy-start(f32[4,1024,256]{2,1,0:T(8,128)} %get-tuple-element.23) | copy-start | bytes 12582916
  212.2 6.6 %copy-start.3 = (f32[4,1024,256]{2,1,0:T(8,128)S(1)}, f32[4,1024,256]{2,1,0:T(8,128)}, u32[]{:S(2)}) copy-start(f32[4,1024,256]{2,1,0:T(8,128)} %copy-done.2) | copy-start | bytes 12582916
  212.2 6.6 %copy-start.6 = (f32[4,1024,256]{2,1,0:T(8,128)S(1)}, f32[4,1024,256]{2,1,0:T(8,128)}, u32[]{:S(2)}) copy-start(f32[4,1024,256]{2,1,0:T(8,128)} %gather_fusion) | copy-start | bytes 12582916
  212.2 16.3 %collective-permute-start.3 = (f32[4,1024,256]{2,1,0:T(8,128)}, f32[4,1024,256]{2,1,0:T(8,128)}, u32[]{:S(2)}, u32[]{:S(2)}) collective-permute-start(f32[4,1024,256]{2,1,0:T(8,128)} %fusion.1), channel_id=1, source_target_pairs={{0,1},{1,0},{2,3},{3,2},{4,5},{5,4},{6,7},{7,6},{8,9},{9,8},{10,11... | collective-permute-start | bytes 12582920 | tf_op jit(solution)/shard_map/ppermute | solution.py:10
  243.9 39.7 %copy-start.1 = (f32[4,256,256]{2,1,0:T(8,128)S(1)}, f32[4,256,256]{2,1,0:T(8,128)}, u32[]{:S(2)}) copy-start(f32[4,256,256]{2,1,0:T(8,128)} %param.13) | copy-start | bytes 3145732
Sparse Core Ops, SparseCore 0:
  227.6 51.8 all-reduce.2
where the time goes:
time: 291 us; the launch traced here: 290 us
  waiting for transfers between devices  165 us (57%)
  matrix products  38.3 us (13%)
  local copies, waits for them, and re-layouts  38.2 us (13%)
  other arithmetic  28 us (10%)
  between operations  14.2 us (5%)
  starting transfers between devices  6.24 us (2%)
    ppermute x4, waiting for transfers between devices, from_partner(): return lax.ppermute(value, axis, pairs)  138 us
    psum x1, waiting for transfers between devices, local(): grad_one, grad_two = lax.psum((counts_one, counts_two), 'batch')  27.6 us
    dot_general x2, matrix products, descend(): jnp.einsum('nbo,noi->nbi', ratio, weight, precision=lax.Precision.HIGHEST)  14.9 us
    dot_general x2, matrix products, descend(): jnp.einsum('nbo,nbi->noi', ratio, scaled, precision=lax.Precision.HIGHEST)  13.4 us
    dot_general x2, matrix products, mixture(): jnp.einsum('nbi,noi->nbo', scaled, weight, precision=lax.Precision.HIGHEST)  10 us
    gather x1, local copies, waits for them, and re-layouts, local(): leaf_adjoint = jnp.take(placed_one, jnp.argsort(own_leaf), axis=0)  7.99 us
    select_n x2, other arithmetic, local(): leaf_adjoint = jnp.take(placed_one, jnp.argsort(own_leaf), axis=0)  7.97 us
    concatenate x1, other arithmetic, local(): placed_one = jnp.concatenate([spread_one, returned_one], axis=0)  7.4 us
  transfers between devices with their start and end apart: 5, of which 4 were waited for; matrix products, arithmetic and copies ran while one was open for 17% of the time, Pallas kernels for 0%

commit v1 on v0

v1 whole, which is shorter than its diff:
```python
import functools

import jax
import jax.numpy as jnp
from jax import lax
from jax.experimental import pallas as pl
from jax.experimental.pallas import tpu as pltpu
from jax.sharding import PartitionSpec as P


HIGHEST = lax.Precision.HIGHEST
VMEM_LIMIT = 48 * 1024 * 1024


def from_partner(value, axis, distance):
    mask = 2**distance
    pairs = [(source, source ^ mask) for source in range(lax.axis_size(axis))]
    return lax.ppermute(value, axis, pairs)


def block(shape, select):
    kind, k = select
    if kind == "table":
        return pl.BlockSpec((None,) + shape, lambda i, t: (t[k], 0, 0))
    return pl.BlockSpec((None,) + shape, lambda i, t: (k, 0, 0))


def whole(shape):
    return pl.BlockSpec(shape, lambda i, t: (0, 0))


ANY = pl.BlockSpec(memory_space=pl.ANY)


def slab_spec(rows, k):
    return pl.BlockSpec((1, rows, k), lambda i, t: (0, 0, 0))


def call(kernel, table, operands, in_specs, out_specs, out_shape, cost, aliases=None, scratch=(), grid=(1,)):
    return pl.pallas_call(
        kernel,
        grid_spec=pltpu.PrefetchScalarGridSpec(
            num_scalar_prefetch=1, grid=grid, in_specs=in_specs, out_specs=out_specs,
            scratch_shapes=list(scratch),
        ),
        out_shape=out_shape,
        input_output_aliases=aliases or {},
        compiler_params=pltpu.CompilerParams(vmem_limit_bytes=VMEM_LIMIT),
        cost_estimate=cost,
    )(table, *operands)


def mix_kernel(table, left, right, weight, out, scaled, totals):
    summed = left[...] + right[...]
    peak = jnp.max(summed, axis=1, keepdims=True)
    p = jnp.exp(summed - peak)
    q = lax.dot_general(p, weight[...], (((1,), (1,)), ((), ())), precision=HIGHEST,
                        preferred_element_type=jnp.float32)
    out[...] = peak + jnp.log(q)
    scaled[...] = p
    totals[...] = q


def mix(table, left, left_sel, right, right_sel, weight, weight_sel):
    rows, k = left.shape[1:]
    o = jax.ShapeDtypeStruct((rows, k), jnp.float32)
    cost = pl.CostEstimate(flops=2 * rows * k * k, transcendentals=2 * rows * k,
                           bytes_accessed=4 * (5 * rows * k + k * k))
    return call(mix_kernel, table, (left, right, weight),
                [block((rows, k), left_sel), block((rows, k), right_sel), block((k, k), weight_sel)],
                [whole((rows, k))] * 3, [o, o, o], cost)


def descend_kernel(placing, own_at, table, adjoint, scaled, totals, weight, *rest):
    if placing == 0:
        counts, spread = rest
    elif placing == 1:
        counts, spread, buffer, sems = rest
    else:
        _, counts, spread, buffer, sems = rest
    ratio = adjoint[...] / totals[...]
    p = scaled[...]
    counts[...] = lax.dot_general(ratio, p, (((0,), (0,)), ((), ())), precision=HIGHEST,
                                  preferred_element_type=jnp.float32)
    spread[...] = p * jnp.dot(ratio, weight[...], precision=HIGHEST, preferred_element_type=jnp.float32)
    if placing == 0:
        return
    c = pltpu.make_async_copy(spread, buffer.at[table[own_at]], sems.at[0])
    c.start()
    c.wait()


def descend(table, adjoint, adjoint_sel, scaled, totals, weight, weight_sel,
            buffer_shape=None, own_at=None, buffer=None):
    rows, k = scaled.shape
    cost = pl.CostEstimate(flops=4 * rows * k * k, transcendentals=0,
                           bytes_accessed=4 * (5 * rows * k + 2 * k * k))
    operands = [adjoint, scaled[None], totals[None], weight]
    in_specs = [block((rows, k), adjoint_sel), block((rows, k), ("fixed", 0)),
                block((rows, k), ("fixed", 0)), block((k, k), weight_sel)]
    out_specs = [whole((k, k)), whole((rows, k))]
    out_shape = [jax.ShapeDtypeStruct((k, k), jnp.float32), jax.ShapeDtypeStruct((rows, k), jnp.float32)]
    placing, aliases, scratch = 0, None, ()
    if buffer_shape is not None:
        placing = 1 if buffer is None else 2
        out_specs.append(ANY)
        out_shape.append(jax.ShapeDtypeStruct(buffer_shape, jnp.float32))
        scratch = (pltpu.SemaphoreType.DMA((1,)),)
        if buffer is not None:
            operands.append(buffer)
            in_specs.append(ANY)
            aliases = {len(operands): 2}
    kernel = functools.partial(descend_kernel, placing, own_at)
    return call(kernel, table, operands, in_specs, out_specs, out_shape, cost, aliases, scratch)


def place_kernel(positions, table, *rest):
    sources, buffer, sems = rest[:len(positions)], rest[len(positions) + 1], rest[-1]
    copies = [pltpu.make_async_copy(src, buffer.at[pl.ds(table[at], 1)], sems.at[n])
              for n, (src, at) in enumerate(zip(sources, positions))]
    for c in copies:
        c.start()
    for c in copies:
        c.wait()


def place(table, buffer, slabs, positions):
    rows, k = slabs[0].shape
    n = len(slabs)
    cost = pl.CostEstimate(flops=0, transcendentals=0, bytes_accessed=8 * rows * k * n)
    return call(functools.partial(place_kernel, tuple(positions)), table,
                tuple(slab[None] for slab in slabs) + (buffer,),
                [slab_spec(rows, k)] * n + [ANY], ANY,
                jax.ShapeDtypeStruct(buffer.shape, buffer.dtype), cost, aliases={n + 1: 0},
                scratch=(pltpu.SemaphoreType.DMA((n,)),))


def grads_kernel(table, late, early, out, sems):
    pairs = [(late, j, j) for j in range(late.shape[0])]
    pairs += [(early, j, late.shape[0] + j) for j in range(early.shape[0])]
    copies = [pltpu.make_async_copy(src.at[pl.ds(j, 1)], out.at[pl.ds(table[at], 1)], sems.at[n])
              for n, (src, j, at) in enumerate(pairs)]
    for c in copies:
        c.start()
    for c in copies:
        c.wait()


def place_grads(table, late, early):
    n, k, _ = late.shape
    m = early.shape[0]
    cost = pl.CostEstimate(flops=0, transcendentals=0, bytes_accessed=8 * (n + m) * k * k)
    spec = lambda a: pl.BlockSpec(a.shape, lambda i, t: (0, 0, 0))
    return call(grads_kernel, table, (late, early), [spec(late), spec(early)], ANY,
                jax.ShapeDtypeStruct((n + m, k, k), jnp.float32), cost,
                scratch=(pltpu.SemaphoreType.DMA((n + m,)),))


def copy_kernel(table, source, out):
    out[...] = source[...]


def select(table, array, at, pieces=1):
    rows, k = array.shape[1:]
    part = rows // pieces
    cost = pl.CostEstimate(flops=0, transcendentals=0, bytes_accessed=8 * rows * k)
    return call(copy_kernel, table, (array,),
                [pl.BlockSpec((None, part, k), lambda i, t: (t[at], i, 0))],
                pl.BlockSpec((part, k), lambda i, t: (i, 0)),
                jax.ShapeDtypeStruct((rows, k), jnp.float32), cost, grid=(pieces,))


def batch_sum(x, axis):
    if lax.axis_size(axis) != 4:
        return lax.psum(x, axis)
    me = lax.axis_index(axis)
    low = jnp.bitwise_and(me, 1) == 0
    high = jnp.bitwise_and(me, 2) == 0
    flat = x.reshape(-1, x.shape[-1])
    half = flat.shape[0] // 2
    a, b = flat[:half], flat[half:]
    got = from_partner(jnp.where(low, b, a), axis, 0)
    keep = jnp.where(low, a, b) + got
    quarter = half // 2
    c, d = keep[:quarter], keep[quarter:]
    got = from_partner(jnp.where(high, d, c), axis, 1)
    mine = jnp.where(high, c, d) + got
    theirs = from_partner(mine, axis, 1)
    keep = jnp.where(high, jnp.concatenate([mine, theirs]), jnp.concatenate([theirs, mine]))
    theirs = from_partner(keep, axis, 0)
    flat = jnp.where(low, jnp.concatenate([keep, theirs]), jnp.concatenate([theirs, keep]))
    return flat.reshape(x.shape)


def local(leaves, leaf_order, node_order, weight_one, weight_two, top_adjoint):
    here = lax.axis_index("region")
    across = jnp.bitwise_xor(here, jnp.int32(1))
    first = weight_one.shape[0]
    second = weight_two.shape[0]
    own_leaf = lax.dynamic_index_in_dim(leaf_order, here, 0, keepdims=False)
    own_node = lax.dynamic_index_in_dim(node_order, here, 0, keepdims=False)
    other_node = lax.dynamic_index_in_dim(node_order, across, 0, keepdims=False)
    rotate = jnp.array(list(range(second, first)) + list(range(second)), jnp.int32)
    perm = own_node[rotate]
    partner_perm = other_node[rotate]
    left_pos = own_leaf[perm]
    send_pos = own_leaf[first + partner_perm]
    table = jnp.concatenate([perm, left_pos, send_pos]).astype(jnp.int32)

    recv_leaf = []
    for s in range(first):
        message = select(table, leaves, 2 * first + s)
        recv_leaf.append(from_partner(message, "region", 0))

    level_one, scaled_one, totals_one, sent_one = [], [], [], []
    for s in range(first):
        out, scaled, totals = mix(table, leaves, ("table", first + s), recv_leaf[s][None], ("fixed", 0),
                                  weight_one, ("table", s))
        level_one.append(out)
        scaled_one.append(scaled)
        totals_one.append(totals)
        if s < second:
            sent_one.append(from_partner(out, "region", 1))

    top_log, counts_two = [], []
    adjoint_one = [None] * first
    for j in range(second):
        out, scaled, totals = mix(table, level_one[second + j][None], ("fixed", 0), sent_one[j][None],
                                  ("fixed", 0), weight_two, ("fixed", j))
        top_log.append(out)
        counts, spread = descend(table, top_adjoint, ("fixed", j), scaled, totals, weight_two, ("fixed", j))
        counts_two.append(counts)
        adjoint_one[second + j] = spread
        adjoint_one[j] = from_partner(spread, "region", 1)

    order = list(range(second, first)) + list(range(second))
    counts_one = [None] * first
    returned = [None] * first
    leaf_adjoint = None
    for s in order:
        counts, spread, leaf_adjoint = descend(
            table, adjoint_one[s][None], ("fixed", 0), scaled_one[s], totals_one[s], weight_one,
            ("table", s), buffer_shape=leaves.shape, own_at=first + s, buffer=leaf_adjoint)
        counts_one[s] = counts
        returned[s] = from_partner(spread, "region", 0)
    leaf_adjoint = place(table, leaf_adjoint, [returned[s] for s in order], [2 * first + s for s in order])
    early = batch_sum(jnp.stack(counts_two + [counts_one[s] for s in range(second, first)]), "batch")
    grad_two = early[:second]
    early = (grad_two, early[second:])
    late = batch_sum(jnp.stack([counts_one[s] for s in range(second)]), "batch")
    grad_one = place_grads(table, late, early[1])
    return (jnp.stack(top_log), leaf_adjoint, grad_one, grad_two)


def solution(mesh):
    return jax.shard_map(
        local,
        mesh=mesh,
        in_specs=(
            P("region", "batch", None),
            P(),
            P(),
            P("region", None, None),
            P("region", None, None),
            P("region", "batch", None),
        ),
        out_specs=(
            P("region", "batch", None),
            P("region", "batch", None),
            P("region", None, None),
            P("region", None, None),
        ),
        check_vma=False,
    )
```

time: 291 us -> 166 us (0.57)
  the two profiles are of different devices: /device:TPU:1 before, /device:TPU:16 now
where the time goes in v1:
time: 166 us; the launch traced here: 165 us
  waiting for transfers between devices  70 us (42%)
  Pallas kernels  59.9 us (36%)
  starting transfers between devices  14.6 us (9%)
  local copies, waits for them, and re-layouts  14.1 us (8%)
  other arithmetic  5.06 us (3%)
    ppermute x20, waiting for transfers between devices, from_partner(): return lax.ppermute(value, axis, pairs)  70 us
    pallas_call x18, Pallas kernels, call(): pl.pallas_call(kernel, grid_spec=pltpu.PrefetchScalarGridSpec(num_scalar_...  59.9 us
    ppermute x20, starting transfers between devices, from_partner(): return lax.ppermute(value, axis, pairs)  14.6 us
    unnamed x46, local copies, waits for them, and re-layouts  9.54 us
  transfers between devices with their start and end apart: 20, of which 10 were waited for; matrix products, arithmetic and copies ran while one was open for 3% of the time, Pallas kernels for 34%

profile of v1, /device:TPU:16, one launch (start us, length us, event | category | flops | bytes accessed | tf_op | source)
XLA Modules:
  0.0 164.8 jit_solution(6494835659362844525)
XLA Ops:
  1.5 1.0 dynamic-slice_reduce_fusion.2
  5.2 1.8 %shard_map.104 = f32[1024,256]{1,0:T(8,128)S(1)} custom-call(s32[12]{0:T(128)S(1)} %pad_add_fusion.table, f32[8,1024,256]{2,1,0:T(8,128)} %left.7), custom_call_target="tpu_custom_call" | custom-call | bytes 2097152 | tf_op jit(solution)/shard_map/pallas_call | solution.py:40
  7.1 1.8 %shard_map.109 = f32[1024,256]{1,0:T(8,128)S(1)} custom-call(s32[12]{0:T(128)S(1)} %pad_add_fusion.table, f32[8,1024,256]{2,1,0:T(8,128)} %left.7), custom_call_target="tpu_custom_call" | custom-call | bytes 2097152 | tf_op jit(solution)/shard_map/pallas_call | solution.py:40
  9.5 2.8 %shard_map.107 = f32[1024,256]{1,0:T(8,128)} custom-call(s32[12]{0:T(128)S(1)} %pad_add_fusion.table, f32[8,1024,256]{2,1,0:T(8,128)} %left.7), custom_call_target="tpu_custom_call" | custom-call | bytes 2097152 | tf_op jit(solution)/shard_map/pallas_call | solution.py:40
  12.3 2.8 %shard_map.102 = f32[1024,256]{1,0:T(8,128)} custom-call(s32[12]{0:T(128)S(1)} %pad_add_fusion.table, f32[8,1024,256]{2,1,0:T(8,128)} %left.7), custom_call_target="tpu_custom_call" | custom-call | bytes 2097152 | tf_op jit(solution)/shard_map/pallas_call | solution.py:40
  15.6 3.9 %shard_map.105 = (f32[1024,256]{1,0:T(8,128)}, f32[1024,256]{1,0:T(8,128)S(1)}, f32[1024,256]{1,0:T(8,128)S(1)}) custom-call(s32[12]{0:T(128)S(1)} %pad_add_fusion.table, f32[8,1024,256]{2,1,0:T(8,128)} %left.7, f32[1,1024,256]{2,1,0:T(8,128)S(1)} %bitcast.73, f32[4,256,256]{2,1,0:T(8,128)S(1)} %copy-done.2), custom_call_target="tpu_custom_call" | custom-call | flops 134217728 | bytes 5505024 | tf_op jit(solution)/shard_map/pallas_call | solution.py:40
  19.6 1.9 %collective-permute-start.2 = (f32[1024,256]{1,0:T(8,128)}, f32[1024,256]{1,0:T(8,128)}, u32[]{:S(2)}, u32[]{:S(2)}) collective-permute-start(f32[1024,256]{1,0:T(8,128)} %get-tuple-element.39), channel_id=1, source_target_pairs={{0,2},{1,3},{2,0},{3,1},{4,6},{5,7},{6,4},{7,5},{8,10},{9,11},{10,... | collective-permute-start | bytes 3145736 | tf_op jit(solution)/shard_map/ppermute | solution.py:18
  21.5 3.9 %shard_map.110 = (f32[1024,256]{1,0:T(8,128)}, f32[1024,256]{1,0:T(8,128)S(1)}, f32[1024,256]{1,0:T(8,128)S(1)}) custom-call(s32[12]{0:T(128)S(1)} %pad_add_fusion.table, f32[8,1024,256]{2,1,0:T(8,128)} %left.7, f32[1,1024,256]{2,1,0:T(8,128)S(1)} %bitcast.72, f32[4,256,256]{2,1,0:T(8,128)S(1)} %copy-done.2), custom_call_target="tpu_custom_call" | custom-call | flops 134217728 | bytes 5505024 | tf_op jit(solution)/shard_map/pallas_call | solution.py:40
  25.4 1.0 copy-done.5
  26.4 1.0 copy-done.7
  27.5 3.2 %shard_map.108 = (f32[1024,256]{1,0:T(8,128)S(1)}, f32[1024,256]{1,0:T(8,128)S(1)}, f32[1024,256]{1,0:T(8,128)S(1)}) custom-call(s32[12]{0:T(128)S(1)} %pad_add_fusion.table, f32[8,1024,256]{2,1,0:T(8,128)} %left.7, f32[1,1024,256]{2,1,0:T(8,128)} %bitcast.10.right, f32[4,256,256]{2,1,0:T(8,128)S(1)} %copy-done.2), custom_call_target="tpu_custom_call" | custom-call | flops 134217728 | bytes 5505024 | tf_op jit(solution)/shard_map/pallas_call | solution.py:40
  30.7 1.0 copy-done.13
  31.6 3.3 %shard_map.103 = (f32[1024,256]{1,0:T(8,128)S(1)}, f32[1024,256]{1,0:T(8,128)S(1)}, f32[1024,256]{1,0:T(8,128)S(1)}) custom-call(s32[12]{0:T(128)S(1)} %pad_add_fusion.table, f32[8,1024,256]{2,1,0:T(8,128)} %left.7, f32[1,1024,256]{2,1,0:T(8,128)} %bitcast.5.right, f32[4,256,256]{2,1,0:T(8,128)S(1)} %copy-done.2), custom_call_target="tpu_custom_call" | custom-call | flops 134217728 | bytes 5505024 | tf_op jit(solution)/shard_map/pallas_call | solution.py:40
  34.9 11.0 %collective-permute-done.2 = f32[1024,256]{1,0:T(8,128)} collective-permute-done((f32[1024,256]{1,0:T(8,128)}, f32[1024,256]{1,0:T(8,128)}, u32[]{:S(2)}, u32[]{:S(2)}) %collective-permute-start.2) | collective-permute-done | bytes 1048608 | tf_op jit(solution)/shard_map/ppermute | solution.py:18
  45.9 2.9 %shard_map.106 = (f32[1024,256]{1,0:T(8,128)S(1)}, f32[1024,256]{1,0:T(8,128)S(1)}, f32[1024,256]{1,0:T(8,128)S(1)}) custom-call(s32[12]{0:T(128)S(1)} %pad_add_fusion.table, f32[1,1024,256]{2,1,0:T(8,128)S(1)} %bitcast.69, f32[1,1024,256]{2,1,0:T(8,128)} %bitcast.8.right, f32[2,256,256]{2,1,0:T(8,128)S(1)} %copy-done.4), custom_call_target="tpu_custom_call" | custom-call | flops 134217728 | bytes 5505024 | tf_op jit(solution)/shard_map/pallas_call | solution.py:40
  48.8 1.0 copy-done.9
  49.8 1.6 copy-done.10
  51.4 3.6 %shard_map.112 = (f32[256,256]{1,0:T(8,128)S(1)}, f32[1024,256]{1,0:T(8,128)}) custom-call(s32[12]{0:T(128)S(1)} %pad_add_fusion.table, f32[2,1024,256]{2,1,0:T(8,128)S(1)} %copy-done.3, f32[1,1024,256]{2,1,0:T(8,128)S(1)} %bitcast.64, f32[1,1024,256]{2,1,0:T(8,128)S(1)} %bitcast.65, f32[2,256,256]{2,1,0:T(8,128)S(1)} %copy-done.4), custom_call_target="tpu_custom_call" | custom-call | flops 268435456 | bytes 5767168 | tf_op jit(solution)/shard_map/pallas_call | solution.py:40
  55.0 1.9 %collective-permute-start.8 = (f32[1024,256]{1,0:T(8,128)}, f32[1024,256]{1,0:T(8,128)}, u32[]{:S(2)}, u32[]{:S(2)}) collective-permute-start(f32[1024,256]{1,0:T(8,128)} %get-tuple-element.46), channel_id=1, source_target_pairs={{0,2},{1,3},{2,0},{3,1},{4,6},{5,7},{6,4},{7,5},{8,10},{9,11},{10,... | collective-permute-start | bytes 3145736 | tf_op jit(solution)/shard_map/ppermute | solution.py:18
  56.9 11.5 %collective-permute-done.5 = f32[1024,256]{1,0:T(8,128)} collective-permute-done((f32[1024,256]{1,0:T(8,128)}, f32[1024,256]{1,0:T(8,128)}, u32[]{:S(2)}, u32[]{:S(2)}) %collective-permute-start.5) | collective-permute-done | bytes 1048608 | tf_op jit(solution)/shard_map/ppermute | solution.py:18
  68.4 1.2 copy-done.14
  69.6 2.9 %shard_map.111 = (f32[1024,256]{1,0:T(8,128)S(1)}, f32[1024,256]{1,0:T(8,128)S(1)}, f32[1024,256]{1,0:T(8,128)S(1)}) custom-call(s32[12]{0:T(128)S(1)} %pad_add_fusion.table, f32[1,1024,256]{2,1,0:T(8,128)S(1)} %bitcast.68, f32[1,1024,256]{2,1,0:T(8,128)} %bitcast.13.right, f32[2,256,256]{2,1,0:T(8,128)S(1)} %copy-done.4), custom_call_target="tpu_custom_call" | custom-call | flops 134217728 | bytes 5505024 | tf_op jit(solution)/shard_map/pallas_call | solution.py:40
  72.5 1.0 copy-done.11
  73.5 1.6 copy-done.12
  75.1 3.6 %shard_map.114 = (f32[256,256]{1,0:T(8,128)S(1)}, f32[1024,256]{1,0:T(8,128)}) custom-call(s32[12]{0:T(128)S(1)} %pad_add_fusion.table, f32[2,1024,256]{2,1,0:T(8,128)S(1)} %copy-done.3, f32[1,1024,256]{2,1,0:T(8,128)S(1)} %bitcast.66, f32[1,1024,256]{2,1,0:T(8,128)S(1)} %bitcast.67, f32[2,256,256]{2,1,0:T(8,128)S(1)} %copy-done.4), custom_call_target="tpu_custom_call" | custom-call | flops 268435456 | bytes 5767168 | tf_op jit(solution)/shard_map/pallas_call | solution.py:40
  78.6 4.8 %shard_map.113 = (f32[256,256]{1,0:T(8,128)S(1)}, f32[1024,256]{1,0:T(8,128)S(1)}, f32[8,1024,256]{2,1,0:T(8,128)}) custom-call(s32[12]{0:T(128)S(1)} %pad_add_fusion.table, f32[1,1024,256]{2,1,0:T(8,128)} %bitcast.17.adjoint, f32[1,1024,256]{2,1,0:T(8,128)S(1)} %bitcast.62, f32[1,1024,256]{2,1,0:T(8,128)S(1)} %bitcast.63, f32[4,256,256]{2,1,0:T(8,128)S(1)} %copy-done.2), custom_call_target="tpu_custom_call" | custom-call | flops 268435456 | bytes 5767168 | tf_op jit(solution)/shard_map/pallas_call | solution.py:40
  83.4 4.8 %shard_map.115 = (f32[256,256]{1,0:T(8,128)S(1)}, f32[1024,256]{1,0:T(8,128)S(1)}, f32[8,1024,256]{2,1,0:T(8,128)}) custom-call(s32[12]{0:T(128)S(1)} %pad_add_fusion.table, f32[1,1024,256]{2,1,0:T(8,128)} %bitcast.23.adjoint, f32[1,1024,256]{2,1,0:T(8,128)S(1)} %bitcast.60, f32[1,1024,256]{2,1,0:T(8,128)S(1)} %bitcast.61, ...), custom_call_target="tpu_custom_call", output_to_operand_aliasing={{2}: (5, {})} | custom-call | flops 268435456 | bytes 5767168 | tf_op jit(solution)/shard_map/pallas_call | solution.py:40
  88.2 1.2 fusion.1
  89.5 1.3 collective-permute-start.16
  90.8 1.9 %collective-permute-start.10 = (f32[1024,256]{1,0:T(8,128)}, f32[1024,256]{1,0:T(8,128)}, u32[]{:S(2)}, u32[]{:S(2)}) collective-permute-start(f32[1024,256]{1,0:T(8,128)} %get-tuple-element.52), channel_id=1, source_target_pairs={{0,2},{1,3},{2,0},{3,1},{4,6},{5,7},{6,4},{7,5},{8,10},{9,11},{10,... | collective-permute-start | bytes 3145736 | tf_op jit(solution)/shard_map/ppermute | solution.py:18
  92.8 9.5 %collective-permute-done.16 = f32[512,256]{1,0:T(8,128)} collective-permute-done((f32[512,256]{1,0:T(8,128)}, f32[512,256]{1,0:T(8,128)}, u32[]{:S(2)}, u32[]{:S(2)}) %collective-permute-start.16) | collective-permute-done | bytes 524320 | tf_op jit(solution)/shard_map/ppermute | solution.py:18
  102.3 1.3 bitcast_add_fusion
  104.3 4.7 %shard_map.116 = (f32[256,256]{1,0:T(8,128)S(1)}, f32[1024,256]{1,0:T(8,128)S(1)}, f32[8,1024,256]{2,1,0:T(8,128)}) custom-call(s32[12]{0:T(128)S(1)} %pad_add_fusion.table, f32[1,1024,256]{2,1,0:T(8,128)} %bitcast.27.adjoint, f32[1,1024,256]{2,1,0:T(8,128)S(1)} %bitcast.52, f32[1,1024,256]{2,1,0:T(8,128)S(1)} %bitcast.53, ...), custom_call_target="tpu_custom_call", output_to_operand_aliasing={{2}: (5, {})} | custom-call | flops 268435456 | bytes 5767168 | tf_op jit(solution)/shard_map/pallas_call | solution.py:40
  109.0 5.5 %collective-permute-done.10 = f32[1024,256]{1,0:T(8,128)} collective-permute-done((f32[1024,256]{1,0:T(8,128)}, f32[1024,256]{1,0:T(8,128)}, u32[]{:S(2)}, u32[]{:S(2)}) %collective-permute-start.10) | collective-permute-done | bytes 1048608 | tf_op jit(solution)/shard_map/ppermute | solution.py:18
  114.5 5.0 %shard_map.117 = (f32[256,256]{1,0:T(8,128)S(1)}, f32[1024,256]{1,0:T(8,128)S(1)}, f32[8,1024,256]{2,1,0:T(8,128)}) custom-call(s32[12]{0:T(128)S(1)} %pad_add_fusion.table, f32[1,1024,256]{2,1,0:T(8,128)} %bitcast.31.adjoint, f32[1,1024,256]{2,1,0:T(8,128)S(1)} %bitcast.54, f32[1,1024,256]{2,1,0:T(8,128)S(1)} %bitcast.55, ...), custom_call_target="tpu_custom_call", output_to_operand_aliasing={{2}: (5, {})} | custom-call | flops 268435456 | bytes 5767168 | tf_op jit(solution)/shard_map/pallas_call | solution.py:40
  119.6 0.8 collective-permute-start.12
  121.0 7.9 %collective-permute-done.12 = f32[256,256]{1,0:T(8,128)S(1)} collective-permute-done((f32[256,256]{1,0:T(8,128)S(1)}, f32[256,256]{1,0:T(8,128)S(1)}, u32[]{:S(2)}, u32[]{:S(2)}) %collective-permute-start.12) | collective-permute-done | bytes 262176 | tf_op jit(solution)/shard_map/ppermute | solution.py:18
  129.7 2.9 %collective-permute-done.18 = f32[256,256]{1,0:T(8,128)S(1)} collective-permute-done((f32[256,256]{1,0:T(8,128)S(1)}, f32[256,256]{1,0:T(8,128)S(1)}, u32[]{:S(2)}, u32[]{:S(2)}) %collective-permute-start.18) | collective-permute-done | bytes 262176 | tf_op jit(solution)/shard_map/ppermute | solution.py:18
  132.6 1.9 %collective-permute-start.19 = (f32[512,256]{1,0:T(8,128)S(1)}, f32[512,256]{1,0:T(8,128)S(1)}, u32[]{:S(2)}, u32[]{:S(2)}) collective-permute-start(f32[512,256]{1,0:T(8,128)S(1)} %maximum_select_fusion.2), channel_id=1, source_target_pairs={{0,32},{32,0},{64,96},{96,64},{1,33},{33,1},{65,97},{97,65},{2,34}... | collective-permute-start | bytes 1572872 | tf_op jit(solution)/shard_map/ppermute | solution.py:18
  135.1 1.8 %collective-permute-done.13 = f32[128,256]{1,0:T(8,128)S(1)} collective-permute-done((f32[128,256]{1,0:T(8,128)S(1)}, f32[128,256]{1,0:T(8,128)S(1)}, u32[]{:S(2)}, u32[]{:S(2)}) %collective-permute-start.13) | collective-permute-done | bytes 131104 | tf_op jit(solution)/shard_map/ppermute | solution.py:18
  136.9 1.5 pad_maximum_fusion
  138.4 8.0 %collective-permute-done.19 = f32[512,256]{1,0:T(8,128)S(1)} collective-permute-done((f32[512,256]{1,0:T(8,128)S(1)}, f32[512,256]{1,0:T(8,128)S(1)}, u32[]{:S(2)}, u32[]{:S(2)}) %collective-permute-start.19) | collective-permute-done | bytes 524320 | tf_op jit(solution)/shard_map/ppermute | solution.py:18
  146.5 7.4 %collective-permute-done.14 = f32[128,256]{1,0:T(8,128)S(1)} collective-permute-done((f32[128,256]{1,0:T(8,128)S(1)}, f32[128,256]{1,0:T(8,128)S(1)}, u32[]{:S(2)}, u32[]{:S(2)}) %collective-permute-start.14) | collective-permute-done | bytes 131104 | tf_op jit(solution)/shard_map/ppermute | solution.py:18
  154.0 1.1 collective-permute-start.15
  155.0 0.9 fusion.4
  155.9 4.5 %collective-permute-done.15 = f32[256,256]{1,0:T(8,128)S(1)} collective-permute-done((f32[256,256]{1,0:T(8,128)S(1)}, f32[256,256]{1,0:T(8,128)S(1)}, u32[]{:S(2)}, u32[]{:S(2)}) %collective-permute-start.15) | collective-permute-done | bytes 262176 | tf_op jit(solution)/shard_map/ppermute | solution.py:18
  160.5 1.5 shard_map.119
  162.1 2.6 %shard_map.118 = f32[8,1024,256]{2,1,0:T(8,128)} custom-call(s32[12]{0:T(128)S(1)} %pad_add_fusion.table, f32[1,1024,256]{2,1,0:T(8,128)S(1)} %bitcast.56, f32[1,1024,256]{2,1,0:T(8,128)S(1)} %bitcast.57, f32[1,1024,256]{2,1,0:T(8,128)S(1)} %bitcast.58, f32[1,1024,256]{2,1,0:T(8,128)S(1)} %bitcast.59, ...), custom_call_target="tpu_custom_call", output_to_operand_aliasing={{}: (5, {})} | custom-call | bytes 8388608 | tf_op jit(solution)/shard_map/pallas_call | solution.py:40
  (81 shorter events, 8.0 us)
Async XLA Ops:
  0.6 0.7 copy-start
  7.0 8.6 %collective-permute-start.1 = (f32[1024,256]{1,0:T(8,128)S(1)}, f32[1024,256]{1,0:T(8,128)S(1)}, u32[]{:S(2)}, u32[]{:S(2)}) collective-permute-start(f32[1024,256]{1,0:T(8,128)S(1)} %shard_map.104), channel_id=1, source_target_pairs={{0,1},{1,0},{2,3},{3,2},{4,5},{5,4},{6,7},{7,6},{8,9},{9,8},{10,11... | collective-permute-start | bytes 3145736 | tf_op jit(solution)/shard_map/ppermute | solution.py:18
  8.9 6.7 %copy-start.2 = (f32[4,256,256]{2,1,0:T(8,128)S(1)}, f32[4,256,256]{2,1,0:T(8,128)}, u32[]{:S(2)}) copy-start(f32[4,256,256]{2,1,0:T(8,128)} %weight.23) | copy-start | bytes 3145732
  8.9 12.5 %collective-permute-start.4 = (f32[1024,256]{1,0:T(8,128)S(1)}, f32[1024,256]{1,0:T(8,128)S(1)}, u32[]{:S(2)}, u32[]{:S(2)}) collective-permute-start(f32[1024,256]{1,0:T(8,128)S(1)} %shard_map.109), channel_id=1, source_target_pairs={{0,1},{1,0},{2,3},{3,2},{4,5},{5,4},{6,7},{7,6},{8,9},{9,8},{10,11... | collective-permute-start | bytes 3145736 | tf_op jit(solution)/shard_map/ppermute | solution.py:18
  12.3 15.1 %collective-permute-start.3 = (f32[1024,256]{1,0:T(8,128)}, f32[1024,256]{1,0:T(8,128)}, u32[]{:S(2)}, u32[]{:S(2)}) collective-permute-start(f32[1024,256]{1,0:T(8,128)} %shard_map.107), channel_id=1, source_target_pairs={{0,1},{1,0},{2,3},{3,2},{4,5},{5,4},{6,7},{7,6},{8,9},{9,8},{10,11... | collective-permute-start | bytes 3145736 | tf_op jit(solution)/shard_map/ppermute | solution.py:18
  15.1 16.5 %collective-permute-start = (f32[1024,256]{1,0:T(8,128)}, f32[1024,256]{1,0:T(8,128)}, u32[]{:S(2)}, u32[]{:S(2)}) collective-permute-start(f32[1024,256]{1,0:T(8,128)} %shard_map.102), channel_id=1, source_target_pairs={{0,1},{1,0},{2,3},{3,2},{4,5},{5,4},{6,7},{7,6},{8,9},{9,8},{10,11... | collective-permute-start | bytes 3145736 | tf_op jit(solution)/shard_map/ppermute | solution.py:18
  19.6 26.3 %collective-permute-start.2 = (f32[1024,256]{1,0:T(8,128)}, f32[1024,256]{1,0:T(8,128)}, u32[]{:S(2)}, u32[]{:S(2)}) collective-permute-start(f32[1024,256]{1,0:T(8,128)} %get-tuple-element.39), channel_id=1, source_target_pairs={{0,2},{1,3},{2,0},{3,1},{4,6},{5,7},{6,4},{7,5},{8,10},{9,11},{10,... | collective-permute-start | bytes 3145736 | tf_op jit(solution)/shard_map/ppermute | solution.py:18
  25.4 1.0 copy-start.5
  26.4 1.0 copy-start.7
  27.4 41.0 %collective-permute-start.5 = (f32[1024,256]{1,0:T(8,128)}, f32[1024,256]{1,0:T(8,128)}, u32[]{:S(2)}, u32[]{:S(2)}) collective-permute-start(f32[1024,256]{1,0:T(8,128)} %get-tuple-element.42), channel_id=1, source_target_pairs={{0,2},{1,3},{2,0},{3,1},{4,6},{5,7},{6,4},{7,5},{8,10},{9,11},{10,... | collective-permute-start | bytes 3145736 | tf_op jit(solution)/shard_map/ppermute | solution.py:18
  27.5 18.4 %copy-start.4 = (f32[2,256,256]{2,1,0:T(8,128)S(1)}, f32[2,256,256]{2,1,0:T(8,128)}, u32[]{:S(2)}) copy-start(f32[2,256,256]{2,1,0:T(8,128)} %weight.20) | copy-start | bytes 1572868
  30.7 1.0 copy-start.13
  31.6 18.2 %copy-start.3 = (f32[2,1024,256]{2,1,0:T(8,128)S(1)}, f32[2,1024,256]{2,1,0:T(8,128)}, u32[]{:S(2)}) copy-start(f32[2,1024,256]{2,1,0:T(8,128)} %adjoint.3) | copy-start | bytes 6291460
  48.8 1.0 copy-start.9
  49.8 18.6 %copy-start.15 = (f32[1024,256]{1,0:T(8,128)}, f32[1024,256]{1,0:T(8,128)S(1)}, u32[]{:S(2)}) copy-start(f32[1024,256]{1,0:T(8,128)S(1)} %get-tuple-element.40) | copy-start | bytes 3145732
  49.8 1.6 copy-start.10
  55.0 49.4 %collective-permute-start.8 = (f32[1024,256]{1,0:T(8,128)}, f32[1024,256]{1,0:T(8,128)}, u32[]{:S(2)}, u32[]{:S(2)}) collective-permute-start(f32[1024,256]{1,0:T(8,128)} %get-tuple-element.46), channel_id=1, source_target_pairs={{0,2},{1,3},{2,0},{3,1},{4,6},{5,7},{6,4},{7,5},{8,10},{9,11},{10,... | collective-permute-start | bytes 3145736 | tf_op jit(solution)/shard_map/ppermute | solution.py:18
  68.4 1.2 copy-start.14
  72.5 1.0 copy-start.11
  73.5 14.7 %copy-start.17 = (f32[1024,256]{1,0:T(8,128)}, f32[1024,256]{1,0:T(8,128)S(1)}, u32[]{:S(2)}) copy-start(f32[1024,256]{1,0:T(8,128)S(1)} %get-tuple-element.43) | copy-start | bytes 3145732
  73.5 1.6 copy-start.12
  83.4 6.0 %copy-start.19 = (f32[1024,256]{1,0:T(8,128)}, f32[1024,256]{1,0:T(8,128)S(1)}, u32[]{:S(2)}) copy-start(f32[1024,256]{1,0:T(8,128)S(1)} %get-tuple-element.49) | copy-start | bytes 3145732
  88.2 1.3 copy-start.21
  89.5 12.7 %collective-permute-start.16 = (f32[512,256]{1,0:T(8,128)}, f32[512,256]{1,0:T(8,128)}, u32[]{:S(2)}, u32[]{:S(2)}) collective-permute-start(f32[512,256]{1,0:T(8,128)} %bitcast.41), channel_id=1, source_target_pairs={{0,32},{32,0},{64,96},{96,64},{1,33},{33,1},{65,97},{97,65},{2,34}... | collective-permute-start | bytes 1572872 | tf_op jit(solution)/shard_map/ppermute | solution.py:18
  90.8 23.7 %collective-permute-start.10 = (f32[1024,256]{1,0:T(8,128)}, f32[1024,256]{1,0:T(8,128)}, u32[]{:S(2)}, u32[]{:S(2)}) collective-permute-start(f32[1024,256]{1,0:T(8,128)} %get-tuple-element.52), channel_id=1, source_target_pairs={{0,2},{1,3},{2,0},{3,1},{4,6},{5,7},{6,4},{7,5},{8,10},{9,11},{10,... | collective-permute-start | bytes 3145736 | tf_op jit(solution)/shard_map/ppermute | solution.py:18
  92.8 21.7 %copy-start.6 = (f32[1024,256]{1,0:T(8,128)S(1)}, f32[1024,256]{1,0:T(8,128)}, u32[]{:S(2)}) copy-start(f32[1024,256]{1,0:T(8,128)} %copy-done.5) | copy-start | bytes 3145732
  92.8 21.7 %copy-start.8 = (f32[1024,256]{1,0:T(8,128)S(1)}, f32[1024,256]{1,0:T(8,128)}, u32[]{:S(2)}) copy-start(f32[1024,256]{1,0:T(8,128)} %copy-done.7) | copy-start | bytes 3145732
  103.6 16.9 %collective-permute-start.17 = (f32[256,256]{1,0:T(8,128)S(1)}, f32[256,256]{1,0:T(8,128)S(1)}, u32[]{:S(2)}, u32[]{:S(2)}) collective-permute-start(f32[256,256]{1,0:T(8,128)S(1)} %slice_select_fusion), channel_id=1, source_target_pairs={{0,64},{32,96},{64,0},{96,32},{1,65},{33,97},{65,1},{97,33},{2,66}... | collective-permute-start | bytes 786440 | tf_op jit(solution)/shard_map/ppermute | solution.py:18
  114.5 20.0 %copy-start.20 = (f32[1024,256]{1,0:T(8,128)S(1)}, f32[1024,256]{1,0:T(8,128)}, u32[]{:S(2)}) copy-start(f32[1024,256]{1,0:T(8,128)} %copy-done.19) | copy-start | bytes 3145732
  114.5 20.0 %copy-start.22 = (f32[1024,256]{1,0:T(8,128)S(1)}, f32[1024,256]{1,0:T(8,128)}, u32[]{:S(2)}) copy-start(f32[1024,256]{1,0:T(8,128)} %copy-done.21) | copy-start | bytes 3145732
  114.5 22.4 %copy-start.16 = (f32[1024,256]{1,0:T(8,128)S(1)}, f32[1024,256]{1,0:T(8,128)}, u32[]{:S(2)}) copy-start(f32[1024,256]{1,0:T(8,128)} %copy-done.15) | copy-start | bytes 3145732
  114.5 22.4 %copy-start.18 = (f32[1024,256]{1,0:T(8,128)S(1)}, f32[1024,256]{1,0:T(8,128)}, u32[]{:S(2)}) copy-start(f32[1024,256]{1,0:T(8,128)} %copy-done.17) | copy-start | bytes 3145732
  119.6 9.3 %collective-permute-start.12 = (f32[256,256]{1,0:T(8,128)S(1)}, f32[256,256]{1,0:T(8,128)S(1)}, u32[]{:S(2)}, u32[]{:S(2)}) collective-permute-start(f32[256,256]{1,0:T(8,128)S(1)} %broadcast_select_fusion), channel_id=1, source_target_pairs={{0,32},{32,0},{64,96},{96,64},{1,33},{33,1},{65,97},{97,65},{2,34}... | collective-permute-start | bytes 786440 | tf_op jit(solution)/shard_map/ppermute | solution.py:18
  120.5 12.1 %collective-permute-start.18 = (f32[256,256]{1,0:T(8,128)S(1)}, f32[256,256]{1,0:T(8,128)S(1)}, u32[]{:S(2)}, u32[]{:S(2)}) collective-permute-start(f32[256,256]{1,0:T(8,128)S(1)} %select_add_fusion), channel_id=1, source_target_pairs={{0,64},{32,96},{64,0},{96,32},{1,65},{33,97},{65,1},{97,33},{2,66}... | collective-permute-start | bytes 786440 | tf_op jit(solution)/shard_map/ppermute | solution.py:18
  129.0 8.0 %collective-permute-start.13 = (f32[128,256]{1,0:T(8,128)S(1)}, f32[128,256]{1,0:T(8,128)S(1)}, u32[]{:S(2)}, u32[]{:S(2)}) collective-permute-start(f32[128,256]{1,0:T(8,128)S(1)} %slice_select_fusion.1), channel_id=1, source_target_pairs={{0,64},{32,96},{64,0},{96,32},{1,65},{33,97},{65,1},{97,33},{2,66}... | collective-permute-start | bytes 393224 | tf_op jit(solution)/shard_map/ppermute | solution.py:18
  132.6 13.8 %collective-permute-start.19 = (f32[512,256]{1,0:T(8,128)S(1)}, f32[512,256]{1,0:T(8,128)S(1)}, u32[]{:S(2)}, u32[]{:S(2)}) collective-permute-start(f32[512,256]{1,0:T(8,128)S(1)} %maximum_select_fusion.2), channel_id=1, source_target_pairs={{0,32},{32,0},{64,96},{96,64},{1,33},{33,1},{65,97},{97,65},{2,34}... | collective-permute-start | bytes 1572872 | tf_op jit(solution)/shard_map/ppermute | solution.py:18
  134.5 27.5 %collective-permute-start.6 = (f32[1024,256]{1,0:T(8,128)S(1)}, f32[1024,256]{1,0:T(8,128)S(1)}, u32[]{:S(2)}, u32[]{:S(2)}) collective-permute-start(f32[1024,256]{1,0:T(8,128)S(1)} %copy-done.20), channel_id=1, source_target_pairs={{0,1},{1,0},{2,3},{3,2},{4,5},{5,4},{6,7},{7,6},{8,9},{9,8},{10,11... | collective-permute-start | bytes 3145736 | tf_op jit(solution)/shard_map/ppermute | solution.py:18
  134.5 27.5 %collective-permute-start.7 = (f32[1024,256]{1,0:T(8,128)S(1)}, f32[1024,256]{1,0:T(8,128)S(1)}, u32[]{:S(2)}, u32[]{:S(2)}) collective-permute-start(f32[1024,256]{1,0:T(8,128)S(1)} %copy-done.22), channel_id=1, source_target_pairs={{0,1},{1,0},{2,3},{3,2},{4,5},{5,4},{6,7},{7,6},{8,9},{9,8},{10,11... | collective-permute-start | bytes 3145736 | tf_op jit(solution)/shard_map/ppermute | solution.py:18
  135.0 27.0 %collective-permute-start.9 = (f32[1024,256]{1,0:T(8,128)S(1)}, f32[1024,256]{1,0:T(8,128)S(1)}, u32[]{:S(2)}, u32[]{:S(2)}) collective-permute-start(f32[1024,256]{1,0:T(8,128)S(1)} %get-tuple-element.60), channel_id=1, source_target_pairs={{0,1},{1,0},{2,3},{3,2},{4,5},{5,4},{6,7},{7,6},{8,9},{9,8},{10,11... | collective-permute-start | bytes 3145736 | tf_op jit(solution)/shard_map/ppermute | solution.py:18
  136.9 25.1 %collective-permute-start.11 = (f32[1024,256]{1,0:T(8,128)S(1)}, f32[1024,256]{1,0:T(8,128)S(1)}, u32[]{:S(2)}, u32[]{:S(2)}) collective-permute-start(f32[1024,256]{1,0:T(8,128)S(1)} %get-tuple-element.64), channel_id=1, source_target_pairs={{0,1},{1,0},{2,3},{3,2},{4,5},{5,4},{6,7},{7,6},{8,9},{9,8},{10,11... | collective-permute-start | bytes 3145736 | tf_op jit(solution)/shard_map/ppermute | solution.py:18
  146.4 7.5 %collective-permute-start.14 = (f32[128,256]{1,0:T(8,128)S(1)}, f32[128,256]{1,0:T(8,128)S(1)}, u32[]{:S(2)}, u32[]{:S(2)}) collective-permute-start(f32[128,256]{1,0:T(8,128)S(1)} %select_add_fusion.2), channel_id=1, source_target_pairs={{0,64},{32,96},{64,0},{96,32},{1,65},{33,97},{65,1},{97,33},{2,66}... | collective-permute-start | bytes 393224 | tf_op jit(solution)/shard_map/ppermute | solution.py:18
  154.0 6.5 %collective-permute-start.15 = (f32[256,256]{1,0:T(8,128)S(1)}, f32[256,256]{1,0:T(8,128)S(1)}, u32[]{:S(2)}, u32[]{:S(2)}) collective-permute-start(f32[256,256]{1,0:T(8,128)S(1)} %maximum_select_fusion.3), channel_id=1, source_target_pairs={{0,32},{32,0},{64,96},{96,64},{1,33},{33,1},{65,97},{97,65},{2,34}... | collective-permute-start | bytes 786440 | tf_op jit(solution)/shard_map/ppermute | solution.py:18
  162.1 2.6 %copy-start.1 = (s32[32,8]{0,1:T(8,128)S(1)}, s32[32,8]{0,1:T(8,128)}, u32[]{:S(2)}) copy-start(s32[32,8]{0,1:T(8,128)} %param.8) | copy-start | bytes 3076

commit v2 on v1

--- a/solution.py
+++ b/solution.py
@@ -23,6 +23,16 @@
     if kind == "table":
         return pl.BlockSpec((None,) + shape, lambda i, t: (t[k], 0, 0))
     return pl.BlockSpec((None,) + shape, lambda i, t: (k, 0, 0))
+
+
+def rows_block(part, k, select):
+    kind, n = select
+    if kind == "table":
+        return pl.BlockSpec((None, part, k), lambda i, t: (t[n], i, 0))
+    return pl.BlockSpec((None, part, k), lambda i, t: (n, i, 0))
+
+
+PIECES = 4
 
 
 def whole(shape):
@@ -63,12 +73,13 @@
 
 def mix(table, left, left_sel, right, right_sel, weight, weight_sel):
     rows, k = left.shape[1:]
+    part = rows // PIECES
     o = jax.ShapeDtypeStruct((rows, k), jnp.float32)
     cost = pl.CostEstimate(flops=2 * rows * k * k, transcendentals=2 * rows * k,
                            bytes_accessed=4 * (5 * rows * k + k * k))
     return call(mix_kernel, table, (left, right, weight),
-                [block((rows, k), left_sel), block((rows, k), right_sel), block((k, k), weight_sel)],
-                [whole((rows, k))] * 3, [o, o, o], cost)
+                [rows_block(part, k, left_sel), rows_block(part, k, right_sel), block((k, k), weight_sel)],
+                [pl.BlockSpec((part, k), lambda i, t: (i, 0))] * 3, [o, o, o], cost, grid=(PIECES,))
 
 
 def descend_kernel(placing, own_at, table, adjoint, scaled, totals, weight, *rest):
@@ -78,14 +89,25 @@
         counts, spread, buffer, sems = rest
     else:
         _, counts, spread, buffer, sems = rest
+    i = pl.program_id(0)
     ratio = adjoint[...] / totals[...]
     p = scaled[...]
-    counts[...] = lax.dot_general(ratio, p, (((0,), (0,)), ((), ())), precision=HIGHEST,
-                                  preferred_element_type=jnp.float32)
+    part = lax.dot_general(ratio, p, (((0,), (0,)), ((), ())), precision=HIGHEST,
+                           preferred_element_type=jnp.float32)
+
+    @pl.when(i == 0)
+    def _():
+        counts[...] = part
+
+    @pl.when(i > 0)
+    def _():
+        counts[...] += part
+
     spread[...] = p * jnp.dot(ratio, weight[...], precision=HIGHEST, preferred_element_type=jnp.float32)
     if placing == 0:
         return
-    c = pltpu.make_async_copy(spread, buffer.at[table[own_at]], sems.at[0])
+    rows = spread.shape[0]
+    c = pltpu.make_async_copy(spread, buffer.at[table[own_at], pl.ds(i * rows, rows)], sems.at[0])
     c.start()
     c.wait()
 
@@ -93,12 +115,13 @@
 def descend(table, adjoint, adjoint_sel, scaled, totals, weight, weight_sel,
             buffer_shape=None, own_at=None, buffer=None):
     rows, k = scaled.shape
+    part = rows // PIECES
     cost = pl.CostEstimate(flops=4 * rows * k * k, transcendentals=0,
                            bytes_accessed=4 * (5 * rows * k + 2 * k * k))
     operands = [adjoint, scaled[None], totals[None], weight]
-    in_specs = [block((rows, k), adjoint_sel), block((rows, k), ("fixed", 0)),
-                block((rows, k), ("fixed", 0)), block((k, k), weight_sel)]
-    out_specs = [whole((k, k)), whole((rows, k))]
+    in_specs = [rows_block(part, k, adjoint_sel), rows_block(part, k, ("fixed", 0)),
+                rows_block(part, k, ("fixed", 0)), block((k, k), weight_sel)]
+    out_specs = [whole((k, k)), pl.BlockSpec((part, k), lambda i, t: (i, 0))]
     out_shape = [jax.ShapeDtypeStruct((k, k), jnp.float32), jax.ShapeDtypeStruct((rows, k), jnp.float32)]
     placing, aliases, scratch = 0, None, ()
     if buffer_shape is not None:
@@ -111,7 +134,8 @@
             in_specs.append(ANY)
             aliases = {len(operands): 2}
     kernel = functools.partial(descend_kernel, placing, own_at)
-    return call(kernel, table, operands, in_specs, out_specs, out_shape, cost, aliases, scratch)
+    return call(kernel, table, operands, in_specs, out_specs, out_shape, cost, aliases, scratch,
+                grid=(PIECES,))
 
 
 def place_kernel(positions, table, *rest):

time: 166 us -> 185 us (1.11)
  the two profiles are of different devices: /device:TPU:16 before, /device:TPU:0 now
where the time goes in v2:
time: 185 us; the launch traced here: 184 us
  Pallas kernels  87.5 us (47%)
  waiting for transfers between devices  56.1 us (30%)
  starting transfers between devices  20.3 us (11%)
  local copies, waits for them, and re-layouts  14.1 us (8%)
  other arithmetic  5.06 us (3%)
    pallas_call x18, Pallas kernels, call(): pl.pallas_call(kernel, grid_spec=pltpu.PrefetchScalarGridSpec(num_scalar_...  87.5 us
    ppermute x20, waiting for transfers between devices, from_partner(): return lax.ppermute(value, axis, pairs)  56.1 us
    ppermute x20, starting transfers between devices, from_partner(): return lax.ppermute(value, axis, pairs)  20.3 us
    unnamed x46, local copies, waits for them, and re-layouts  9.55 us
  transfers between devices with their start and end apart: 20, of which 9 were waited for; matrix products, arithmetic and copies ran while one was open for 3% of the time, Pallas kernels for 45%

profile of v2, /device:TPU:0, one launch (start us, length us, event | category | flops | bytes accessed | tf_op | source)
XLA Modules:
  0.0 184.2 jit_solution(231084506761841235)
XLA Ops:
  1.5 1.0 dynamic-slice_reduce_fusion.2
  5.2 1.8 shard_map.104
  7.1 1.8 shard_map.109
  9.5 2.8 %shard_map.107 = f32[1024,256]{1,0:T(8,128)} custom-call(s32[12]{0:T(128)S(1)} %pad_add_fusion.table, f32[8,1024,256]{2,1,0:T(8,128)} %left.7), custom_call_target="tpu_custom_call" | custom-call | bytes 2097152 | tf_op jit(solution)/shard_map/pallas_call | solution.py:50
  12.3 2.8 %shard_map.102 = f32[1024,256]{1,0:T(8,128)} custom-call(s32[12]{0:T(128)S(1)} %pad_add_fusion.table, f32[8,1024,256]{2,1,0:T(8,128)} %left.7), custom_call_target="tpu_custom_call" | custom-call | bytes 2097152 | tf_op jit(solution)/shard_map/pallas_call | solution.py:50
  15.6 4.8 %shard_map.105 = (f32[1024,256]{1,0:T(8,128)}, f32[1024,256]{1,0:T(8,128)S(1)}, f32[1024,256]{1,0:T(8,128)S(1)}) custom-call(s32[12]{0:T(128)S(1)} %pad_add_fusion.table, f32[8,1024,256]{2,1,0:T(8,128)} %left.7, f32[1,1024,256]{2,1,0:T(8,128)S(1)} %bitcast.73, f32[4,256,256]{2,1,0:T(8,128)S(1)} %copy-done.2), custom_call_target="tpu_custom_call" | custom-call | flops 134217728 | bytes 5505024 | tf_op jit(solution)/shard_map/pallas_call | solution.py:50
  20.4 2.0 %collective-permute-start.2 = (f32[1024,256]{1,0:T(8,128)}, f32[1024,256]{1,0:T(8,128)}, u32[]{:S(2)}, u32[]{:S(2)}) collective-permute-start(f32[1024,256]{1,0:T(8,128)} %get-tuple-element.39), channel_id=1, source_target_pairs={{0,2},{1,3},{2,0},{3,1},{4,6},{5,7},{6,4},{7,5},{8,10},{9,11},{10,... | collective-permute-start | bytes 3145736 | tf_op jit(solution)/shard_map/ppermute | solution.py:18
  22.5 4.8 %shard_map.110 = (f32[1024,256]{1,0:T(8,128)}, f32[1024,256]{1,0:T(8,128)S(1)}, f32[1024,256]{1,0:T(8,128)S(1)}) custom-call(s32[12]{0:T(128)S(1)} %pad_add_fusion.table, f32[8,1024,256]{2,1,0:T(8,128)} %left.7, f32[1,1024,256]{2,1,0:T(8,128)S(1)} %bitcast.72, f32[4,256,256]{2,1,0:T(8,128)S(1)} %copy-done.2), custom_call_target="tpu_custom_call" | custom-call | flops 134217728 | bytes 5505024 | tf_op jit(solution)/shard_map/pallas_call | solution.py:50
  27.3 1.0 copy-done.5
  28.2 1.0 copy-done.7
  29.2 4.0 %shard_map.108 = (f32[1024,256]{1,0:T(8,128)S(1)}, f32[1024,256]{1,0:T(8,128)S(1)}, f32[1024,256]{1,0:T(8,128)S(1)}) custom-call(s32[12]{0:T(128)S(1)} %pad_add_fusion.table, f32[8,1024,256]{2,1,0:T(8,128)} %left.7, f32[1,1024,256]{2,1,0:T(8,128)} %bitcast.10.right, f32[4,256,256]{2,1,0:T(8,128)S(1)} %copy-done.2), custom_call_target="tpu_custom_call" | custom-call | flops 134217728 | bytes 5505024 | tf_op jit(solution)/shard_map/pallas_call | solution.py:50
  33.3 1.0 copy-done.13
  34.3 4.1 %shard_map.103 = (f32[1024,256]{1,0:T(8,128)S(1)}, f32[1024,256]{1,0:T(8,128)S(1)}, f32[1024,256]{1,0:T(8,128)S(1)}) custom-call(s32[12]{0:T(128)S(1)} %pad_add_fusion.table, f32[8,1024,256]{2,1,0:T(8,128)} %left.7, f32[1,1024,256]{2,1,0:T(8,128)} %bitcast.5.right, f32[4,256,256]{2,1,0:T(8,128)S(1)} %copy-done.2), custom_call_target="tpu_custom_call" | custom-call | flops 134217728 | bytes 5505024 | tf_op jit(solution)/shard_map/pallas_call | solution.py:50
  38.4 8.4 %collective-permute-done.2 = f32[1024,256]{1,0:T(8,128)} collective-permute-done((f32[1024,256]{1,0:T(8,128)}, f32[1024,256]{1,0:T(8,128)}, u32[]{:S(2)}, u32[]{:S(2)}) %collective-permute-start.2) | collective-permute-done | bytes 1048608 | tf_op jit(solution)/shard_map/ppermute | solution.py:18
  46.8 3.9 %shard_map.106 = (f32[1024,256]{1,0:T(8,128)S(1)}, f32[1024,256]{1,0:T(8,128)S(1)}, f32[1024,256]{1,0:T(8,128)S(1)}) custom-call(s32[12]{0:T(128)S(1)} %pad_add_fusion.table, f32[1,1024,256]{2,1,0:T(8,128)S(1)} %bitcast.69, f32[1,1024,256]{2,1,0:T(8,128)} %bitcast.8.right, f32[2,256,256]{2,1,0:T(8,128)S(1)} %copy-done.4), custom_call_target="tpu_custom_call" | custom-call | flops 134217728 | bytes 5505024 | tf_op jit(solution)/shard_map/pallas_call | solution.py:50
  50.7 1.0 copy-done.9
  51.7 1.6 copy-done.10
  53.3 6.1 %shard_map.112 = (f32[256,256]{1,0:T(8,128)S(1)}, f32[1024,256]{1,0:T(8,128)}) custom-call(s32[12]{0:T(128)S(1)} %pad_add_fusion.table, f32[2,1024,256]{2,1,0:T(8,128)S(1)} %copy-done.3, f32[1,1024,256]{2,1,0:T(8,128)S(1)} %bitcast.64, f32[1,1024,256]{2,1,0:T(8,128)S(1)} %bitcast.65, f32[2,256,256]{2,1,0:T(8,128)S(1)} %copy-done.4), custom_call_target="tpu_custom_call" | custom-call | flops 268435456 | bytes 5767168 | tf_op jit(solution)/shard_map/pallas_call | solution.py:50
  59.3 2.0 %collective-permute-start.8 = (f32[1024,256]{1,0:T(8,128)}, f32[1024,256]{1,0:T(8,128)}, u32[]{:S(2)}, u32[]{:S(2)}) collective-permute-start(f32[1024,256]{1,0:T(8,128)} %get-tuple-element.46), channel_id=1, source_target_pairs={{0,2},{1,3},{2,0},{3,1},{4,6},{5,7},{6,4},{7,5},{8,10},{9,11},{10,... | collective-permute-start | bytes 3145736 | tf_op jit(solution)/shard_map/ppermute | solution.py:18
  61.3 7.9 %collective-permute-done.5 = f32[1024,256]{1,0:T(8,128)} collective-permute-done((f32[1024,256]{1,0:T(8,128)}, f32[1024,256]{1,0:T(8,128)}, u32[]{:S(2)}, u32[]{:S(2)}) %collective-permute-start.5) | collective-permute-done | bytes 1048608 | tf_op jit(solution)/shard_map/ppermute | solution.py:18
  69.3 1.2 copy-done.14
  70.5 3.9 %shard_map.111 = (f32[1024,256]{1,0:T(8,128)S(1)}, f32[1024,256]{1,0:T(8,128)S(1)}, f32[1024,256]{1,0:T(8,128)S(1)}) custom-call(s32[12]{0:T(128)S(1)} %pad_add_fusion.table, f32[1,1024,256]{2,1,0:T(8,128)S(1)} %bitcast.68, f32[1,1024,256]{2,1,0:T(8,128)} %bitcast.13.right, f32[2,256,256]{2,1,0:T(8,128)S(1)} %copy-done.4), custom_call_target="tpu_custom_call" | custom-call | flops 134217728 | bytes 5505024 | tf_op jit(solution)/shard_map/pallas_call | solution.py:50
  74.4 1.0 copy-done.11
  75.3 1.6 copy-done.12
  77.0 6.0 %shard_map.114 = (f32[256,256]{1,0:T(8,128)S(1)}, f32[1024,256]{1,0:T(8,128)}) custom-call(s32[12]{0:T(128)S(1)} %pad_add_fusion.table, f32[2,1024,256]{2,1,0:T(8,128)S(1)} %copy-done.3, f32[1,1024,256]{2,1,0:T(8,128)S(1)} %bitcast.66, f32[1,1024,256]{2,1,0:T(8,128)S(1)} %bitcast.67, f32[2,256,256]{2,1,0:T(8,128)S(1)} %copy-done.4), custom_call_target="tpu_custom_call" | custom-call | flops 268435456 | bytes 5767168 | tf_op jit(solution)/shard_map/pallas_call | solution.py:50
  83.0 9.1 %shard_map.113 = (f32[256,256]{1,0:T(8,128)S(1)}, f32[1024,256]{1,0:T(8,128)S(1)}, f32[8,1024,256]{2,1,0:T(8,128)}) custom-call(s32[12]{0:T(128)S(1)} %pad_add_fusion.table, f32[1,1024,256]{2,1,0:T(8,128)} %bitcast.17.adjoint, f32[1,1024,256]{2,1,0:T(8,128)S(1)} %bitcast.62, f32[1,1024,256]{2,1,0:T(8,128)S(1)} %bitcast.63, f32[4,256,256]{2,1,0:T(8,128)S(1)} %copy-done.2), custom_call_target="tpu_custom_call" | custom-call | flops 268435456 | bytes 5767168 | tf_op jit(solution)/shard_map/pallas_call | solution.py:50
  92.1 9.1 %shard_map.115 = (f32[256,256]{1,0:T(8,128)S(1)}, f32[1024,256]{1,0:T(8,128)S(1)}, f32[8,1024,256]{2,1,0:T(8,128)}) custom-call(s32[12]{0:T(128)S(1)} %pad_add_fusion.table, f32[1,1024,256]{2,1,0:T(8,128)} %bitcast.23.adjoint, f32[1,1024,256]{2,1,0:T(8,128)S(1)} %bitcast.60, f32[1,1024,256]{2,1,0:T(8,128)S(1)} %bitcast.61, ...), custom_call_target="tpu_custom_call", output_to_operand_aliasing={{2}: (5, {})} | custom-call | flops 268435456 | bytes 5767168 | tf_op jit(solution)/shard_map/pallas_call | solution.py:50
  101.2 1.2 fusion.1
  102.5 1.7 collective-permute-start.16
  104.2 1.9 %collective-permute-start.10 = (f32[1024,256]{1,0:T(8,128)}, f32[1024,256]{1,0:T(8,128)}, u32[]{:S(2)}, u32[]{:S(2)}) collective-permute-start(f32[1024,256]{1,0:T(8,128)} %get-tuple-element.52), channel_id=1, source_target_pairs={{0,2},{1,3},{2,0},{3,1},{4,6},{5,7},{6,4},{7,5},{8,10},{9,11},{10,... | collective-permute-start | bytes 3145736 | tf_op jit(solution)/shard_map/ppermute | solution.py:18
  106.1 9.3 %collective-permute-done.16 = f32[512,256]{1,0:T(8,128)} collective-permute-done((f32[512,256]{1,0:T(8,128)}, f32[512,256]{1,0:T(8,128)}, u32[]{:S(2)}, u32[]{:S(2)}) %collective-permute-start.16) | collective-permute-done | bytes 524320 | tf_op jit(solution)/shard_map/ppermute | solution.py:18
  115.4 1.3 bitcast_add_fusion
  116.7 3.2 %collective-permute-start.17 = (f32[256,256]{1,0:T(8,128)S(1)}, f32[256,256]{1,0:T(8,128)S(1)}, u32[]{:S(2)}, u32[]{:S(2)}) collective-permute-start(f32[256,256]{1,0:T(8,128)S(1)} %slice_select_fusion), channel_id=1, source_target_pairs={{0,64},{32,96},{64,0},{96,32},{1,65},{33,97},{65,1},{97,33},{2,66}... | collective-permute-start | bytes 786440 | tf_op jit(solution)/shard_map/ppermute | solution.py:18
  119.9 9.1 %shard_map.116 = (f32[256,256]{1,0:T(8,128)S(1)}, f32[1024,256]{1,0:T(8,128)S(1)}, f32[8,1024,256]{2,1,0:T(8,128)}) custom-call(s32[12]{0:T(128)S(1)} %pad_add_fusion.table, f32[1,1024,256]{2,1,0:T(8,128)} %bitcast.27.adjoint, f32[1,1024,256]{2,1,0:T(8,128)S(1)} %bitcast.52, f32[1,1024,256]{2,1,0:T(8,128)S(1)} %bitcast.53, ...), custom_call_target="tpu_custom_call", output_to_operand_aliasing={{2}: (5, {})} | custom-call | flops 268435456 | bytes 5767168 | tf_op jit(solution)/shard_map/pallas_call | solution.py:50
  129.0 9.4 %shard_map.117 = (f32[256,256]{1,0:T(8,128)S(1)}, f32[1024,256]{1,0:T(8,128)S(1)}, f32[8,1024,256]{2,1,0:T(8,128)}) custom-call(s32[12]{0:T(128)S(1)} %pad_add_fusion.table, f32[1,1024,256]{2,1,0:T(8,128)} %bitcast.31.adjoint, f32[1,1024,256]{2,1,0:T(8,128)S(1)} %bitcast.54, f32[1,1024,256]{2,1,0:T(8,128)S(1)} %bitcast.55, ...), custom_call_target="tpu_custom_call", output_to_operand_aliasing={{2}: (5, {})} | custom-call | flops 268435456 | bytes 5767168 | tf_op jit(solution)/shard_map/pallas_call | solution.py:50
  139.4 1.9 %collective-permute-start.18 = (f32[256,256]{1,0:T(8,128)S(1)}, f32[256,256]{1,0:T(8,128)S(1)}, u32[]{:S(2)}, u32[]{:S(2)}) collective-permute-start(f32[256,256]{1,0:T(8,128)S(1)} %select_add_fusion), channel_id=1, source_target_pairs={{0,64},{32,96},{64,0},{96,32},{1,65},{33,97},{65,1},{97,33},{2,66}... | collective-permute-start | bytes 786440 | tf_op jit(solution)/shard_map/ppermute | solution.py:18
  141.4 6.5 %collective-permute-done.12 = f32[256,256]{1,0:T(8,128)S(1)} collective-permute-done((f32[256,256]{1,0:T(8,128)S(1)}, f32[256,256]{1,0:T(8,128)S(1)}, u32[]{:S(2)}, u32[]{:S(2)}) %collective-permute-start.12) | collective-permute-done | bytes 262176 | tf_op jit(solution)/shard_map/ppermute | solution.py:18
  148.0 1.8 collective-permute-start.13
  149.8 2.9 %collective-permute-done.18 = f32[256,256]{1,0:T(8,128)S(1)} collective-permute-done((f32[256,256]{1,0:T(8,128)S(1)}, f32[256,256]{1,0:T(8,128)S(1)}, u32[]{:S(2)}, u32[]{:S(2)}) %collective-permute-start.18) | collective-permute-done | bytes 262176 | tf_op jit(solution)/shard_map/ppermute | solution.py:18
  152.7 1.7 collective-permute-start.19
  155.0 1.0 collective-permute-done.13
  155.9 1.5 pad_maximum_fusion
  157.4 8.0 %collective-permute-done.19 = f32[512,256]{1,0:T(8,128)S(1)} collective-permute-done((f32[512,256]{1,0:T(8,128)S(1)}, f32[512,256]{1,0:T(8,128)S(1)}, u32[]{:S(2)}, u32[]{:S(2)}) %collective-permute-start.19) | collective-permute-done | bytes 524320 | tf_op jit(solution)/shard_map/ppermute | solution.py:18
  165.4 1.0 collective-permute-start.14
  166.6 6.7 %collective-permute-done.14 = f32[128,256]{1,0:T(8,128)S(1)} collective-permute-done((f32[128,256]{1,0:T(8,128)S(1)}, f32[128,256]{1,0:T(8,128)S(1)}, u32[]{:S(2)}, u32[]{:S(2)}) %collective-permute-start.14) | collective-permute-done | bytes 131104 | tf_op jit(solution)/shard_map/ppermute | solution.py:18
  174.5 5.3 %collective-permute-done.15 = f32[256,256]{1,0:T(8,128)S(1)} collective-permute-done((f32[256,256]{1,0:T(8,128)S(1)}, f32[256,256]{1,0:T(8,128)S(1)}, u32[]{:S(2)}, u32[]{:S(2)}) %collective-permute-start.15) | collective-permute-done | bytes 262176 | tf_op jit(solution)/shard_map/ppermute | solution.py:18
  179.8 1.5 shard_map.119
  181.4 2.6 %shard_map.118 = f32[8,1024,256]{2,1,0:T(8,128)} custom-call(s32[12]{0:T(128)S(1)} %pad_add_fusion.table, f32[1,1024,256]{2,1,0:T(8,128)S(1)} %bitcast.56, f32[1,1024,256]{2,1,0:T(8,128)S(1)} %bitcast.57, f32[1,1024,256]{2,1,0:T(8,128)S(1)} %bitcast.58, f32[1,1024,256]{2,1,0:T(8,128)S(1)} %bitcast.59, ...), custom_call_target="tpu_custom_call", output_to_operand_aliasing={{}: (5, {})} | custom-call | bytes 8388608 | tf_op jit(solution)/shard_map/pallas_call | solution.py:50
  (81 shorter events, 8.0 us)
Async XLA Ops:
  0.6 0.7 copy-start
  7.0 8.6 %collective-permute-start.1 = (f32[1024,256]{1,0:T(8,128)S(1)}, f32[1024,256]{1,0:T(8,128)S(1)}, u32[]{:S(2)}, u32[]{:S(2)}) collective-permute-start(f32[1024,256]{1,0:T(8,128)S(1)} %shard_map.104), channel_id=1, source_target_pairs={{0,1},{1,0},{2,3},{3,2},{4,5},{5,4},{6,7},{7,6},{8,9},{9,8},{10,11... | collective-permute-start | bytes 3145736 | tf_op jit(solution)/shard_map/ppermute | solution.py:18
  8.9 6.7 %copy-start.2 = (f32[4,256,256]{2,1,0:T(8,128)S(1)}, f32[4,256,256]{2,1,0:T(8,128)}, u32[]{:S(2)}) copy-start(f32[4,256,256]{2,1,0:T(8,128)} %weight.23) | copy-start | bytes 3145732
  8.9 13.5 %collective-permute-start.4 = (f32[1024,256]{1,0:T(8,128)S(1)}, f32[1024,256]{1,0:T(8,128)S(1)}, u32[]{:S(2)}, u32[]{:S(2)}) collective-permute-start(f32[1024,256]{1,0:T(8,128)S(1)} %shard_map.109), channel_id=1, source_target_pairs={{0,1},{1,0},{2,3},{3,2},{4,5},{5,4},{6,7},{7,6},{8,9},{9,8},{10,11... | collective-permute-start | bytes 3145736 | tf_op jit(solution)/shard_map/ppermute | solution.py:18
  12.3 16.9 %collective-permute-start.3 = (f32[1024,256]{1,0:T(8,128)}, f32[1024,256]{1,0:T(8,128)}, u32[]{:S(2)}, u32[]{:S(2)}) collective-permute-start(f32[1024,256]{1,0:T(8,128)} %shard_map.107), channel_id=1, source_target_pairs={{0,1},{1,0},{2,3},{3,2},{4,5},{5,4},{6,7},{7,6},{8,9},{9,8},{10,11... | collective-permute-start | bytes 3145736 | tf_op jit(solution)/shard_map/ppermute | solution.py:18
  15.1 19.1 %collective-permute-start = (f32[1024,256]{1,0:T(8,128)}, f32[1024,256]{1,0:T(8,128)}, u32[]{:S(2)}, u32[]{:S(2)}) collective-permute-start(f32[1024,256]{1,0:T(8,128)} %shard_map.102), channel_id=1, source_target_pairs={{0,1},{1,0},{2,3},{3,2},{4,5},{5,4},{6,7},{7,6},{8,9},{9,8},{10,11... | collective-permute-start | bytes 3145736 | tf_op jit(solution)/shard_map/ppermute | solution.py:18
  20.4 26.4 %collective-permute-start.2 = (f32[1024,256]{1,0:T(8,128)}, f32[1024,256]{1,0:T(8,128)}, u32[]{:S(2)}, u32[]{:S(2)}) collective-permute-start(f32[1024,256]{1,0:T(8,128)} %get-tuple-element.39), channel_id=1, source_target_pairs={{0,2},{1,3},{2,0},{3,1},{4,6},{5,7},{6,4},{7,5},{8,10},{9,11},{10,... | collective-permute-start | bytes 3145736 | tf_op jit(solution)/shard_map/ppermute | solution.py:18
  27.2 1.0 copy-start.5
  28.2 1.0 copy-start.7
  29.2 40.0 %collective-permute-start.5 = (f32[1024,256]{1,0:T(8,128)}, f32[1024,256]{1,0:T(8,128)}, u32[]{:S(2)}, u32[]{:S(2)}) collective-permute-start(f32[1024,256]{1,0:T(8,128)} %get-tuple-element.42), channel_id=1, source_target_pairs={{0,2},{1,3},{2,0},{3,1},{4,6},{5,7},{6,4},{7,5},{8,10},{9,11},{10,... | collective-permute-start | bytes 3145736 | tf_op jit(solution)/shard_map/ppermute | solution.py:18
  29.2 17.6 %copy-start.4 = (f32[2,256,256]{2,1,0:T(8,128)S(1)}, f32[2,256,256]{2,1,0:T(8,128)}, u32[]{:S(2)}) copy-start(f32[2,256,256]{2,1,0:T(8,128)} %weight.20) | copy-start | bytes 1572868
  33.3 1.0 copy-start.13
  34.3 17.4 %copy-start.3 = (f32[2,1024,256]{2,1,0:T(8,128)S(1)}, f32[2,1024,256]{2,1,0:T(8,128)}, u32[]{:S(2)}) copy-start(f32[2,1024,256]{2,1,0:T(8,128)} %adjoint.3) | copy-start | bytes 6291460
  50.7 1.0 copy-start.9
  51.7 17.6 %copy-start.15 = (f32[1024,256]{1,0:T(8,128)}, f32[1024,256]{1,0:T(8,128)S(1)}, u32[]{:S(2)}) copy-start(f32[1024,256]{1,0:T(8,128)S(1)} %get-tuple-element.40) | copy-start | bytes 3145732
  51.7 1.6 copy-start.10
  59.3 60.6 %collective-permute-start.8 = (f32[1024,256]{1,0:T(8,128)}, f32[1024,256]{1,0:T(8,128)}, u32[]{:S(2)}, u32[]{:S(2)}) collective-permute-start(f32[1024,256]{1,0:T(8,128)} %get-tuple-element.46), channel_id=1, source_target_pairs={{0,2},{1,3},{2,0},{3,1},{4,6},{5,7},{6,4},{7,5},{8,10},{9,11},{10,... | collective-permute-start | bytes 3145736 | tf_op jit(solution)/shard_map/ppermute | solution.py:18
  69.3 1.2 copy-start.14
  74.4 1.0 copy-start.11
  75.3 25.8 %copy-start.17 = (f32[1024,256]{1,0:T(8,128)}, f32[1024,256]{1,0:T(8,128)S(1)}, u32[]{:S(2)}) copy-start(f32[1024,256]{1,0:T(8,128)S(1)} %get-tuple-element.43) | copy-start | bytes 3145732
  75.3 1.6 copy-start.12
  92.1 10.3 %copy-start.19 = (f32[1024,256]{1,0:T(8,128)}, f32[1024,256]{1,0:T(8,128)S(1)}, u32[]{:S(2)}) copy-start(f32[1024,256]{1,0:T(8,128)S(1)} %get-tuple-element.49) | copy-start | bytes 3145732
  101.2 1.3 copy-start.21
  102.5 12.9 %collective-permute-start.16 = (f32[512,256]{1,0:T(8,128)}, f32[512,256]{1,0:T(8,128)}, u32[]{:S(2)}, u32[]{:S(2)}) collective-permute-start(f32[512,256]{1,0:T(8,128)} %bitcast.41), channel_id=1, source_target_pairs={{0,32},{32,0},{64,96},{96,64},{1,33},{33,1},{65,97},{97,65},{2,34}... | collective-permute-start | bytes 1572872 | tf_op jit(solution)/shard_map/ppermute | solution.py:18
  104.2 24.8 %collective-permute-start.10 = (f32[1024,256]{1,0:T(8,128)}, f32[1024,256]{1,0:T(8,128)}, u32[]{:S(2)}, u32[]{:S(2)}) collective-permute-start(f32[1024,256]{1,0:T(8,128)} %get-tuple-element.52), channel_id=1, source_target_pairs={{0,2},{1,3},{2,0},{3,1},{4,6},{5,7},{6,4},{7,5},{8,10},{9,11},{10,... | collective-permute-start | bytes 3145736 | tf_op jit(solution)/shard_map/ppermute | solution.py:18
  106.1 22.9 %copy-start.6 = (f32[1024,256]{1,0:T(8,128)S(1)}, f32[1024,256]{1,0:T(8,128)}, u32[]{:S(2)}) copy-start(f32[1024,256]{1,0:T(8,128)} %copy-done.5) | copy-start | bytes 3145732
  106.1 22.9 %copy-start.8 = (f32[1024,256]{1,0:T(8,128)S(1)}, f32[1024,256]{1,0:T(8,128)}, u32[]{:S(2)}) copy-start(f32[1024,256]{1,0:T(8,128)} %copy-done.7) | copy-start | bytes 3145732
  116.7 22.7 %collective-permute-start.17 = (f32[256,256]{1,0:T(8,128)S(1)}, f32[256,256]{1,0:T(8,128)S(1)}, u32[]{:S(2)}, u32[]{:S(2)}) collective-permute-start(f32[256,256]{1,0:T(8,128)S(1)} %slice_select_fusion), channel_id=1, source_target_pairs={{0,64},{32,96},{64,0},{96,32},{1,65},{33,97},{65,1},{97,33},{2,66}... | collective-permute-start | bytes 786440 | tf_op jit(solution)/shard_map/ppermute | solution.py:18
  129.0 25.4 %copy-start.20 = (f32[1024,256]{1,0:T(8,128)S(1)}, f32[1024,256]{1,0:T(8,128)}, u32[]{:S(2)}) copy-start(f32[1024,256]{1,0:T(8,128)} %copy-done.19) | copy-start | bytes 3145732
  129.0 25.4 %copy-start.22 = (f32[1024,256]{1,0:T(8,128)S(1)}, f32[1024,256]{1,0:T(8,128)}, u32[]{:S(2)}) copy-start(f32[1024,256]{1,0:T(8,128)} %copy-done.21) | copy-start | bytes 3145732
  129.0 26.9 %copy-start.16 = (f32[1024,256]{1,0:T(8,128)S(1)}, f32[1024,256]{1,0:T(8,128)}, u32[]{:S(2)}) copy-start(f32[1024,256]{1,0:T(8,128)} %copy-done.15) | copy-start | bytes 3145732
  129.0 26.9 %copy-start.18 = (f32[1024,256]{1,0:T(8,128)S(1)}, f32[1024,256]{1,0:T(8,128)}, u32[]{:S(2)}) copy-start(f32[1024,256]{1,0:T(8,128)} %copy-done.17) | copy-start | bytes 3145732
  138.4 9.4 %collective-permute-start.12 = (f32[256,256]{1,0:T(8,128)S(1)}, f32[256,256]{1,0:T(8,128)S(1)}, u32[]{:S(2)}, u32[]{:S(2)}) collective-permute-start(f32[256,256]{1,0:T(8,128)S(1)} %broadcast_select_fusion), channel_id=1, source_target_pairs={{0,32},{32,0},{64,96},{96,64},{1,33},{33,1},{65,97},{97,65},{2,34}... | collective-permute-start | bytes 786440 | tf_op jit(solution)/shard_map/ppermute | solution.py:18
  139.4 13.2 %collective-permute-start.18 = (f32[256,256]{1,0:T(8,128)S(1)}, f32[256,256]{1,0:T(8,128)S(1)}, u32[]{:S(2)}, u32[]{:S(2)}) collective-permute-start(f32[256,256]{1,0:T(8,128)S(1)} %select_add_fusion), channel_id=1, source_target_pairs={{0,64},{32,96},{64,0},{96,32},{1,65},{33,97},{65,1},{97,33},{2,66}... | collective-permute-start | bytes 786440 | tf_op jit(solution)/shard_map/ppermute | solution.py:18
  148.0 8.0 %collective-permute-start.13 = (f32[128,256]{1,0:T(8,128)S(1)}, f32[128,256]{1,0:T(8,128)S(1)}, u32[]{:S(2)}, u32[]{:S(2)}) collective-permute-start(f32[128,256]{1,0:T(8,128)S(1)} %slice_select_fusion.1), channel_id=1, source_target_pairs={{0,64},{32,96},{64,0},{96,32},{1,65},{33,97},{65,1},{97,33},{2,66}... | collective-permute-start | bytes 393224 | tf_op jit(solution)/shard_map/ppermute | solution.py:18
  152.7 12.7 %collective-permute-start.19 = (f32[512,256]{1,0:T(8,128)S(1)}, f32[512,256]{1,0:T(8,128)S(1)}, u32[]{:S(2)}, u32[]{:S(2)}) collective-permute-start(f32[512,256]{1,0:T(8,128)S(1)} %maximum_select_fusion.2), channel_id=1, source_target_pairs={{0,32},{32,0},{64,96},{96,64},{1,33},{33,1},{65,97},{97,65},{2,34}... | collective-permute-start | bytes 1572872 | tf_op jit(solution)/shard_map/ppermute | solution.py:18
  154.4 27.0 %collective-permute-start.6 = (f32[1024,256]{1,0:T(8,128)S(1)}, f32[1024,256]{1,0:T(8,128)S(1)}, u32[]{:S(2)}, u32[]{:S(2)}) collective-permute-start(f32[1024,256]{1,0:T(8,128)S(1)} %copy-done.20), channel_id=1, source_target_pairs={{0,1},{1,0},{2,3},{3,2},{4,5},{5,4},{6,7},{7,6},{8,9},{9,8},{10,11... | collective-permute-start | bytes 3145736 | tf_op jit(solution)/shard_map/ppermute | solution.py:18
  154.4 27.0 %collective-permute-start.7 = (f32[1024,256]{1,0:T(8,128)S(1)}, f32[1024,256]{1,0:T(8,128)S(1)}, u32[]{:S(2)}, u32[]{:S(2)}) collective-permute-start(f32[1024,256]{1,0:T(8,128)S(1)} %copy-done.22), channel_id=1, source_target_pairs={{0,1},{1,0},{2,3},{3,2},{4,5},{5,4},{6,7},{7,6},{8,9},{9,8},{10,11... | collective-permute-start | bytes 3145736 | tf_op jit(solution)/shard_map/ppermute | solution.py:18
  154.9 26.5 %collective-permute-start.9 = (f32[1024,256]{1,0:T(8,128)S(1)}, f32[1024,256]{1,0:T(8,128)S(1)}, u32[]{:S(2)}, u32[]{:S(2)}) collective-permute-start(f32[1024,256]{1,0:T(8,128)S(1)} %get-tuple-element.60), channel_id=1, source_target_pairs={{0,1},{1,0},{2,3},{3,2},{4,5},{5,4},{6,7},{7,6},{8,9},{9,8},{10,11... | collective-permute-start | bytes 3145736 | tf_op jit(solution)/shard_map/ppermute | solution.py:18
  155.9 25.5 %collective-permute-start.11 = (f32[1024,256]{1,0:T(8,128)S(1)}, f32[1024,256]{1,0:T(8,128)S(1)}, u32[]{:S(2)}, u32[]{:S(2)}) collective-permute-start(f32[1024,256]{1,0:T(8,128)S(1)} %get-tuple-element.64), channel_id=1, source_target_pairs={{0,1},{1,0},{2,3},{3,2},{4,5},{5,4},{6,7},{7,6},{8,9},{9,8},{10,11... | collective-permute-start | bytes 3145736 | tf_op jit(solution)/shard_map/ppermute | solution.py:18
  165.4 7.9 %collective-permute-start.14 = (f32[128,256]{1,0:T(8,128)S(1)}, f32[128,256]{1,0:T(8,128)S(1)}, u32[]{:S(2)}, u32[]{:S(2)}) collective-permute-start(f32[128,256]{1,0:T(8,128)S(1)} %select_add_fusion.2), channel_id=1, source_target_pairs={{0,64},{32,96},{64,0},{96,32},{1,65},{33,97},{65,1},{97,33},{2,66}... | collective-permute-start | bytes 393224 | tf_op jit(solution)/shard_map/ppermute | solution.py:18
  173.3 6.5 %collective-permute-start.15 = (f32[256,256]{1,0:T(8,128)S(1)}, f32[256,256]{1,0:T(8,128)S(1)}, u32[]{:S(2)}, u32[]{:S(2)}) collective-permute-start(f32[256,256]{1,0:T(8,128)S(1)} %maximum_select_fusion.3), channel_id=1, source_target_pairs={{0,32},{32,0},{64,96},{96,64},{1,33},{33,1},{65,97},{97,65},{2,34}... | collective-permute-start | bytes 786440 | tf_op jit(solution)/shard_map/ppermute | solution.py:18
  181.4 2.6 %copy-start.1 = (s32[32,8]{0,1:T(8,128)S(1)}, s32[32,8]{0,1:T(8,128)}, u32[]{:S(2)}) copy-start(s32[32,8]{0,1:T(8,128)} %param.8) | copy-start | bytes 3076

commit v3 on v1

--- a/solution.py
+++ b/solution.py
@@ -197,14 +197,15 @@
     across = jnp.bitwise_xor(here, jnp.int32(1))
     first = weight_one.shape[0]
     second = weight_two.shape[0]
-    own_leaf = lax.dynamic_index_in_dim(leaf_order, here, 0, keepdims=False)
-    own_node = lax.dynamic_index_in_dim(node_order, here, 0, keepdims=False)
-    other_node = lax.dynamic_index_in_dim(node_order, across, 0, keepdims=False)
-    rotate = jnp.array(list(range(second, first)) + list(range(second)), jnp.int32)
-    perm = own_node[rotate]
-    partner_perm = other_node[rotate]
-    left_pos = own_leaf[perm]
-    send_pos = own_leaf[first + partner_perm]
+    regions = jnp.arange(leaf_order.shape[0], dtype=jnp.int32)[:, None]
+    own_leaf = jnp.sum(jnp.where(regions == here, leaf_order, 0), axis=0)
+    own_node = jnp.sum(jnp.where(regions == here, node_order, 0), axis=0)
+    other_node = jnp.sum(jnp.where(regions == across, node_order, 0), axis=0)
+    perm = jnp.concatenate([own_node[second:], own_node[:second]])
+    partner_perm = jnp.concatenate([other_node[second:], other_node[:second]])
+    leaf_slots = jnp.arange(leaf_order.shape[1], dtype=jnp.int32)[None, :]
+    left_pos = jnp.sum(jnp.where(leaf_slots == perm[:, None], own_leaf[None, :], 0), axis=1)
+    send_pos = jnp.sum(jnp.where(leaf_slots == first + partner_perm[:, None], own_leaf[None, :], 0), axis=1)
     table = jnp.concatenate([perm, left_pos, send_pos]).astype(jnp.int32)
 
     recv_leaf = []

time: 166 us -> 163 us (0.982)
  local copies, waits for them, and re-layouts: 14.1 us -> 10.4 us
    gather x4 -> x0, local copies, waits for them, and re-layouts: 2.57 us -> none  [the longest x1 0.65 us: local(): perm = own_node[rotate]]
    reduce_sum x0 -> x3, other arithmetic: none -> 1.85 us  [the longest x1 0.83 us: local(): own_node = jnp.sum(jnp.where(regions == here, node_order, 0), axis=0)]
    unnamed x46 -> x42, local copies, waits for them, and re-layouts: 9.54 us -> 9.49 us
where the time goes in v3:
time: 163 us
  waiting for transfers between devices  70 us (43%)
  Pallas kernels  59.9 us (37%)
  starting transfers between devices  14.6 us (9%)
  local copies, waits for them, and re-layouts  10.4 us (6%)
  other arithmetic  6.43 us (4%)
    ppermute x20, waiting for transfers between devices, from_partner(): return lax.ppermute(value, axis, pairs)  70 us
    pallas_call x18, Pallas kernels, call(): pl.pallas_call(kernel, grid_spec=pltpu.PrefetchScalarGridSpec(num_scalar_...  59.9 us
    ppermute x20, starting transfers between devices, from_partner(): return lax.ppermute(value, axis, pairs)  14.6 us
    unnamed x42, local copies, waits for them, and re-layouts  9.49 us
  transfers between devices with their start and end apart: 20, of which 10 were waited for; matrix products, arithmetic and copies ran while one was open for 3% of the time, Pallas kernels for 34%

profile of v3, /device:TPU:16, one launch (start us, length us, event | category | flops | bytes accessed | tf_op | source)
XLA Modules:
  0.0 162.5 jit_solution(6641430635332175887)
XLA Ops:
  1.5 0.8 select_reduce_fusion.4
  2.8 1.8 %shard_map.95 = f32[1024,256]{1,0:T(8,128)S(1)} custom-call(s32[12]{0:T(128)S(1)} %pad_add_fusion.1.table, f32[8,1024,256]{2,1,0:T(8,128)} %left.7), custom_call_target="tpu_custom_call" | custom-call | bytes 2097152 | tf_op jit(solution)/shard_map/pallas_call | solution.py:40
  4.8 1.8 %shard_map.100 = f32[1024,256]{1,0:T(8,128)S(1)} custom-call(s32[12]{0:T(128)S(1)} %pad_add_fusion.1.table, f32[8,1024,256]{2,1,0:T(8,128)} %left.7), custom_call_target="tpu_custom_call" | custom-call | bytes 2097152 | tf_op jit(solution)/shard_map/pallas_call | solution.py:40
  7.2 2.8 %shard_map.98 = f32[1024,256]{1,0:T(8,128)} custom-call(s32[12]{0:T(128)S(1)} %pad_add_fusion.1.table, f32[8,1024,256]{2,1,0:T(8,128)} %left.7), custom_call_target="tpu_custom_call" | custom-call | bytes 2097152 | tf_op jit(solution)/shard_map/pallas_call | solution.py:40
  10.0 2.8 %shard_map.93 = f32[1024,256]{1,0:T(8,128)} custom-call(s32[12]{0:T(128)S(1)} %pad_add_fusion.1.table, f32[8,1024,256]{2,1,0:T(8,128)} %left.7), custom_call_target="tpu_custom_call" | custom-call | bytes 2097152 | tf_op jit(solution)/shard_map/pallas_call | solution.py:40
  13.3 3.9 %shard_map.96 = (f32[1024,256]{1,0:T(8,128)}, f32[1024,256]{1,0:T(8,128)S(1)}, f32[1024,256]{1,0:T(8,128)S(1)}) custom-call(s32[12]{0:T(128)S(1)} %pad_add_fusion.1.table, f32[8,1024,256]{2,1,0:T(8,128)} %left.7, f32[1,1024,256]{2,1,0:T(8,128)S(1)} %bitcast.63, f32[4,256,256]{2,1,0:T(8,128)S(1)} %copy-done), custom_call_target="tpu_custom_call" | custom-call | flops 134217728 | bytes 5505024 | tf_op jit(solution)/shard_map/pallas_call | solution.py:40
  17.2 1.9 %collective-permute-start.2 = (f32[1024,256]{1,0:T(8,128)}, f32[1024,256]{1,0:T(8,128)}, u32[]{:S(2)}, u32[]{:S(2)}) collective-permute-start(f32[1024,256]{1,0:T(8,128)} %get-tuple-element.39), channel_id=1, source_target_pairs={{0,2},{1,3},{2,0},{3,1},{4,6},{5,7},{6,4},{7,5},{8,10},{9,11},{10,... | collective-permute-start | bytes 3145736 | tf_op jit(solution)/shard_map/ppermute | solution.py:18
  19.2 3.9 %shard_map.101 = (f32[1024,256]{1,0:T(8,128)}, f32[1024,256]{1,0:T(8,128)S(1)}, f32[1024,256]{1,0:T(8,128)S(1)}) custom-call(s32[12]{0:T(128)S(1)} %pad_add_fusion.1.table, f32[8,1024,256]{2,1,0:T(8,128)} %left.7, f32[1,1024,256]{2,1,0:T(8,128)S(1)} %bitcast.62, f32[4,256,256]{2,1,0:T(8,128)S(1)} %copy-done), custom_call_target="tpu_custom_call" | custom-call | flops 134217728 | bytes 5505024 | tf_op jit(solution)/shard_map/pallas_call | solution.py:40
  23.1 1.0 copy-done.3
  24.0 1.0 copy-done.5
  25.1 3.2 %shard_map.99 = (f32[1024,256]{1,0:T(8,128)S(1)}, f32[1024,256]{1,0:T(8,128)S(1)}, f32[1024,256]{1,0:T(8,128)S(1)}) custom-call(s32[12]{0:T(128)S(1)} %pad_add_fusion.1.table, f32[8,1024,256]{2,1,0:T(8,128)} %left.7, f32[1,1024,256]{2,1,0:T(8,128)} %bitcast.5.right, f32[4,256,256]{2,1,0:T(8,128)S(1)} %copy-done), custom_call_target="tpu_custom_call" | custom-call | flops 134217728 | bytes 5505024 | tf_op jit(solution)/shard_map/pallas_call | solution.py:40
  28.3 1.0 copy-done.11
  29.3 3.3 %shard_map.94 = (f32[1024,256]{1,0:T(8,128)S(1)}, f32[1024,256]{1,0:T(8,128)S(1)}, f32[1024,256]{1,0:T(8,128)S(1)}) custom-call(s32[12]{0:T(128)S(1)} %pad_add_fusion.1.table, f32[8,1024,256]{2,1,0:T(8,128)} %left.7, f32[1,1024,256]{2,1,0:T(8,128)} %bitcast.right, f32[4,256,256]{2,1,0:T(8,128)S(1)} %copy-done), custom_call_target="tpu_custom_call" | custom-call | flops 134217728 | bytes 5505024 | tf_op jit(solution)/shard_map/pallas_call | solution.py:40
  32.6 11.0 %collective-permute-done.2 = f32[1024,256]{1,0:T(8,128)} collective-permute-done((f32[1024,256]{1,0:T(8,128)}, f32[1024,256]{1,0:T(8,128)}, u32[]{:S(2)}, u32[]{:S(2)}) %collective-permute-start.2) | collective-permute-done | bytes 1048608 | tf_op jit(solution)/shard_map/ppermute | solution.py:18
  43.6 2.9 %shard_map.97 = (f32[1024,256]{1,0:T(8,128)S(1)}, f32[1024,256]{1,0:T(8,128)S(1)}, f32[1024,256]{1,0:T(8,128)S(1)}) custom-call(s32[12]{0:T(128)S(1)} %pad_add_fusion.1.table, f32[1,1024,256]{2,1,0:T(8,128)S(1)} %bitcast.59, f32[1,1024,256]{2,1,0:T(8,128)} %bitcast.3.right, f32[2,256,256]{2,1,0:T(8,128)S(1)} %copy-done.2), custom_call_target="tpu_custom_call" | custom-call | flops 134217728 | bytes 5505024 | tf_op jit(solution)/shard_map/pallas_call | solution.py:40
  46.5 1.0 copy-done.7
  47.5 1.6 copy-done.8
  49.1 3.6 %shard_map.103 = (f32[256,256]{1,0:T(8,128)S(1)}, f32[1024,256]{1,0:T(8,128)}) custom-call(s32[12]{0:T(128)S(1)} %pad_add_fusion.1.table, f32[2,1024,256]{2,1,0:T(8,128)S(1)} %copy-done.1, f32[1,1024,256]{2,1,0:T(8,128)S(1)} %bitcast.54, f32[1,1024,256]{2,1,0:T(8,128)S(1)} %bitcast.55, f32[2,256,256]{2,1,0:T(8,128)S(1)} %copy-done.2), custom_call_target="tpu_custom_call" | custom-call | flops 268435456 | bytes 5767168 | tf_op jit(solution)/shard_map/pallas_call | solution.py:40
  52.6 1.9 %collective-permute-start.8 = (f32[1024,256]{1,0:T(8,128)}, f32[1024,256]{1,0:T(8,128)}, u32[]{:S(2)}, u32[]{:S(2)}) collective-permute-start(f32[1024,256]{1,0:T(8,128)} %get-tuple-element.46), channel_id=1, source_target_pairs={{0,2},{1,3},{2,0},{3,1},{4,6},{5,7},{6,4},{7,5},{8,10},{9,11},{10,... | collective-permute-start | bytes 3145736 | tf_op jit(solution)/shard_map/ppermute | solution.py:18
  54.6 11.5 %collective-permute-done.5 = f32[1024,256]{1,0:T(8,128)} collective-permute-done((f32[1024,256]{1,0:T(8,128)}, f32[1024,256]{1,0:T(8,128)}, u32[]{:S(2)}, u32[]{:S(2)}) %collective-permute-start.5) | collective-permute-done | bytes 1048608 | tf_op jit(solution)/shard_map/ppermute | solution.py:18
  66.1 1.2 copy-done.12
  67.3 2.9 %shard_map.102 = (f32[1024,256]{1,0:T(8,128)S(1)}, f32[1024,256]{1,0:T(8,128)S(1)}, f32[1024,256]{1,0:T(8,128)S(1)}) custom-call(s32[12]{0:T(128)S(1)} %pad_add_fusion.1.table, f32[1,1024,256]{2,1,0:T(8,128)S(1)} %bitcast.58, f32[1,1024,256]{2,1,0:T(8,128)} %bitcast.8.right, f32[2,256,256]{2,1,0:T(8,128)S(1)} %copy-done.2), custom_call_target="tpu_custom_call" | custom-call | flops 134217728 | bytes 5505024 | tf_op jit(solution)/shard_map/pallas_call | solution.py:40
  70.2 1.0 copy-done.9
  71.2 1.6 copy-done.10
  72.8 3.5 %shard_map.105 = (f32[256,256]{1,0:T(8,128)S(1)}, f32[1024,256]{1,0:T(8,128)}) custom-call(s32[12]{0:T(128)S(1)} %pad_add_fusion.1.table, f32[2,1024,256]{2,1,0:T(8,128)S(1)} %copy-done.1, f32[1,1024,256]{2,1,0:T(8,128)S(1)} %bitcast.56, f32[1,1024,256]{2,1,0:T(8,128)S(1)} %bitcast.57, f32[2,256,256]{2,1,0:T(8,128)S(1)} %copy-done.2), custom_call_target="tpu_custom_call" | custom-call | flops 268435456 | bytes 5767168 | tf_op jit(solution)/shard_map/pallas_call | solution.py:40
  76.3 4.8 %shard_map.104 = (f32[256,256]{1,0:T(8,128)S(1)}, f32[1024,256]{1,0:T(8,128)S(1)}, f32[8,1024,256]{2,1,0:T(8,128)}) custom-call(s32[12]{0:T(128)S(1)} %pad_add_fusion.1.table, f32[1,1024,256]{2,1,0:T(8,128)} %bitcast.12.adjoint, f32[1,1024,256]{2,1,0:T(8,128)S(1)} %bitcast.52, f32[1,1024,256]{2,1,0:T(8,128)S(1)} %bitcast.53, f32[4,256,256]{2,1,0:T(8,128)S(1)} %copy-done), custom_call_target="tpu_custom_call" | custom-call | flops 268435456 | bytes 5767168 | tf_op jit(solution)/shard_map/pallas_call | solution.py:40
  81.1 4.8 %shard_map.106 = (f32[256,256]{1,0:T(8,128)S(1)}, f32[1024,256]{1,0:T(8,128)S(1)}, f32[8,1024,256]{2,1,0:T(8,128)}) custom-call(s32[12]{0:T(128)S(1)} %pad_add_fusion.1.table, f32[1,1024,256]{2,1,0:T(8,128)} %bitcast.18.adjoint, f32[1,1024,256]{2,1,0:T(8,128)S(1)} %bitcast.50, f32[1,1024,256]{2,1,0:T(8,128)S(1)} %bitcast.51, ...), custom_call_target="tpu_custom_call", output_to_operand_aliasing={{2}: (5, {})} | custom-call | flops 268435456 | bytes 5767168 | tf_op jit(solution)/shard_map/pallas_call | solution.py:40
  85.9 1.2 fusion.1
  87.2 1.3 collective-permute-start.16
  88.5 1.9 %collective-permute-start.10 = (f32[1024,256]{1,0:T(8,128)}, f32[1024,256]{1,0:T(8,128)}, u32[]{:S(2)}, u32[]{:S(2)}) collective-permute-start(f32[1024,256]{1,0:T(8,128)} %get-tuple-element.52), channel_id=1, source_target_pairs={{0,2},{1,3},{2,0},{3,1},{4,6},{5,7},{6,4},{7,5},{8,10},{9,11},{10,... | collective-permute-start | bytes 3145736 | tf_op jit(solution)/shard_map/ppermute | solution.py:18
  90.5 9.5 %collective-permute-done.16 = f32[512,256]{1,0:T(8,128)} collective-permute-done((f32[512,256]{1,0:T(8,128)}, f32[512,256]{1,0:T(8,128)}, u32[]{:S(2)}, u32[]{:S(2)}) %collective-permute-start.16) | collective-permute-done | bytes 524320 | tf_op jit(solution)/shard_map/ppermute | solution.py:18
  100.0 1.3 bitcast_add_fusion
  102.0 4.7 %shard_map.107 = (f32[256,256]{1,0:T(8,128)S(1)}, f32[1024,256]{1,0:T(8,128)S(1)}, f32[8,1024,256]{2,1,0:T(8,128)}) custom-call(s32[12]{0:T(128)S(1)} %pad_add_fusion.1.table, f32[1,1024,256]{2,1,0:T(8,128)} %bitcast.22.adjoint, f32[1,1024,256]{2,1,0:T(8,128)S(1)} %bitcast.42, f32[1,1024,256]{2,1,0:T(8,128)S(1)} %bitcast.43, ...), custom_call_target="tpu_custom_call", output_to_operand_aliasing={{2}: (5, {})} | custom-call | flops 268435456 | bytes 5767168 | tf_op jit(solution)/shard_map/pallas_call | solution.py:40
  106.7 5.5 %collective-permute-done.10 = f32[1024,256]{1,0:T(8,128)} collective-permute-done((f32[1024,256]{1,0:T(8,128)}, f32[1024,256]{1,0:T(8,128)}, u32[]{:S(2)}, u32[]{:S(2)}) %collective-permute-start.10) | collective-permute-done | bytes 1048608 | tf_op jit(solution)/shard_map/ppermute | solution.py:18
  112.2 5.0 %shard_map.108 = (f32[256,256]{1,0:T(8,128)S(1)}, f32[1024,256]{1,0:T(8,128)S(1)}, f32[8,1024,256]{2,1,0:T(8,128)}) custom-call(s32[12]{0:T(128)S(1)} %pad_add_fusion.1.table, f32[1,1024,256]{2,1,0:T(8,128)} %bitcast.26.adjoint, f32[1,1024,256]{2,1,0:T(8,128)S(1)} %bitcast.44, f32[1,1024,256]{2,1,0:T(8,128)S(1)} %bitcast.45, ...), custom_call_target="tpu_custom_call", output_to_operand_aliasing={{2}: (5, {})} | custom-call | flops 268435456 | bytes 5767168 | tf_op jit(solution)/shard_map/pallas_call | solution.py:40
  117.3 0.8 collective-permute-start.12
  118.7 7.9 %collective-permute-done.12 = f32[256,256]{1,0:T(8,128)S(1)} collective-permute-done((f32[256,256]{1,0:T(8,128)S(1)}, f32[256,256]{1,0:T(8,128)S(1)}, u32[]{:S(2)}, u32[]{:S(2)}) %collective-permute-start.12) | collective-permute-done | bytes 262176 | tf_op jit(solution)/shard_map/ppermute | solution.py:18
  127.4 2.9 %collective-permute-done.18 = f32[256,256]{1,0:T(8,128)S(1)} collective-permute-done((f32[256,256]{1,0:T(8,128)S(1)}, f32[256,256]{1,0:T(8,128)S(1)}, u32[]{:S(2)}, u32[]{:S(2)}) %collective-permute-start.18) | collective-permute-done | bytes 262176 | tf_op jit(solution)/shard_map/ppermute | solution.py:18
  130.3 1.9 %collective-permute-start.19 = (f32[512,256]{1,0:T(8,128)S(1)}, f32[512,256]{1,0:T(8,128)S(1)}, u32[]{:S(2)}, u32[]{:S(2)}) collective-permute-start(f32[512,256]{1,0:T(8,128)S(1)} %maximum_select_fusion.2), channel_id=1, source_target_pairs={{0,32},{32,0},{64,96},{96,64},{1,33},{33,1},{65,97},{97,65},{2,34}... | collective-permute-start | bytes 1572872 | tf_op jit(solution)/shard_map/ppermute | solution.py:18
  132.8 1.8 %collective-permute-done.13 = f32[128,256]{1,0:T(8,128)S(1)} collective-permute-done((f32[128,256]{1,0:T(8,128)S(1)}, f32[128,256]{1,0:T(8,128)S(1)}, u32[]{:S(2)}, u32[]{:S(2)}) %collective-permute-start.13) | collective-permute-done | bytes 131104 | tf_op jit(solution)/shard_map/ppermute | solution.py:18
  134.6 1.5 pad_maximum_fusion
  136.1 8.0 %collective-permute-done.19 = f32[512,256]{1,0:T(8,128)S(1)} collective-permute-done((f32[512,256]{1,0:T(8,128)S(1)}, f32[512,256]{1,0:T(8,128)S(1)}, u32[]{:S(2)}, u32[]{:S(2)}) %collective-permute-start.19) | collective-permute-done | bytes 524320 | tf_op jit(solution)/shard_map/ppermute | solution.py:18
  144.2 7.4 %collective-permute-done.14 = f32[128,256]{1,0:T(8,128)S(1)} collective-permute-done((f32[128,256]{1,0:T(8,128)S(1)}, f32[128,256]{1,0:T(8,128)S(1)}, u32[]{:S(2)}, u32[]{:S(2)}) %collective-permute-start.14) | collective-permute-done | bytes 131104 | tf_op jit(solution)/shard_map/ppermute | solution.py:18
  151.7 1.1 collective-permute-start.15
  152.7 0.9 fusion.2
  153.6 4.5 %collective-permute-done.15 = f32[256,256]{1,0:T(8,128)S(1)} collective-permute-done((f32[256,256]{1,0:T(8,128)S(1)}, f32[256,256]{1,0:T(8,128)S(1)}, u32[]{:S(2)}, u32[]{:S(2)}) %collective-permute-start.15) | collective-permute-done | bytes 262176 | tf_op jit(solution)/shard_map/ppermute | solution.py:18
  158.2 1.5 shard_map.110
  159.7 2.6 %shard_map.109 = f32[8,1024,256]{2,1,0:T(8,128)} custom-call(s32[12]{0:T(128)S(1)} %pad_add_fusion.1.table, f32[1,1024,256]{2,1,0:T(8,128)S(1)} %bitcast.46, f32[1,1024,256]{2,1,0:T(8,128)S(1)} %bitcast.47, f32[1,1024,256]{2,1,0:T(8,128)S(1)} %bitcast.48, f32[1,1024,256]{2,1,0:T(8,128)S(1)} %bitcast.49, ...), custom_call_target="tpu_custom_call", output_to_operand_aliasing={{}: (5, {})} | custom-call | bytes 8388608 | tf_op jit(solution)/shard_map/pallas_call | solution.py:40
  (75 shorter events, 5.8 us)
Async XLA Ops:
  4.7 8.6 %collective-permute-start.1 = (f32[1024,256]{1,0:T(8,128)S(1)}, f32[1024,256]{1,0:T(8,128)S(1)}, u32[]{:S(2)}, u32[]{:S(2)}) collective-permute-start(f32[1024,256]{1,0:T(8,128)S(1)} %shard_map.95), channel_id=1, source_target_pairs={{0,1},{1,0},{2,3},{3,2},{4,5},{5,4},{6,7},{7,6},{8,9},{9,8},{10,11... | collective-permute-start | bytes 3145736 | tf_op jit(solution)/shard_map/ppermute | solution.py:18
  6.6 6.7 %copy-start = (f32[4,256,256]{2,1,0:T(8,128)S(1)}, f32[4,256,256]{2,1,0:T(8,128)}, u32[]{:S(2)}) copy-start(f32[4,256,256]{2,1,0:T(8,128)} %weight.23) | copy-start | bytes 3145732
  6.6 12.5 %collective-permute-start.4 = (f32[1024,256]{1,0:T(8,128)S(1)}, f32[1024,256]{1,0:T(8,128)S(1)}, u32[]{:S(2)}, u32[]{:S(2)}) collective-permute-start(f32[1024,256]{1,0:T(8,128)S(1)} %shard_map.100), channel_id=1, source_target_pairs={{0,1},{1,0},{2,3},{3,2},{4,5},{5,4},{6,7},{7,6},{8,9},{9,8},{10,11... | collective-permute-start | bytes 3145736 | tf_op jit(solution)/shard_map/ppermute | solution.py:18
  10.0 15.1 %collective-permute-start.3 = (f32[1024,256]{1,0:T(8,128)}, f32[1024,256]{1,0:T(8,128)}, u32[]{:S(2)}, u32[]{:S(2)}) collective-permute-start(f32[1024,256]{1,0:T(8,128)} %shard_map.98), channel_id=1, source_target_pairs={{0,1},{1,0},{2,3},{3,2},{4,5},{5,4},{6,7},{7,6},{8,9},{9,8},{10,11... | collective-permute-start | bytes 3145736 | tf_op jit(solution)/shard_map/ppermute | solution.py:18
  12.8 16.5 %collective-permute-start = (f32[1024,256]{1,0:T(8,128)}, f32[1024,256]{1,0:T(8,128)}, u32[]{:S(2)}, u32[]{:S(2)}) collective-permute-start(f32[1024,256]{1,0:T(8,128)} %shard_map.93), channel_id=1, source_target_pairs={{0,1},{1,0},{2,3},{3,2},{4,5},{5,4},{6,7},{7,6},{8,9},{9,8},{10,11... | collective-permute-start | bytes 3145736 | tf_op jit(solution)/shard_map/ppermute | solution.py:18
  17.2 26.3 %collective-permute-start.2 = (f32[1024,256]{1,0:T(8,128)}, f32[1024,256]{1,0:T(8,128)}, u32[]{:S(2)}, u32[]{:S(2)}) collective-permute-start(f32[1024,256]{1,0:T(8,128)} %get-tuple-element.39), channel_id=1, source_target_pairs={{0,2},{1,3},{2,0},{3,1},{4,6},{5,7},{6,4},{7,5},{8,10},{9,11},{10,... | collective-permute-start | bytes 3145736 | tf_op jit(solution)/shard_map/ppermute | solution.py:18
  23.0 1.0 copy-start.3
  24.0 1.0 copy-start.5
  25.0 41.0 %collective-permute-start.5 = (f32[1024,256]{1,0:T(8,128)}, f32[1024,256]{1,0:T(8,128)}, u32[]{:S(2)}, u32[]{:S(2)}) collective-permute-start(f32[1024,256]{1,0:T(8,128)} %get-tuple-element.42), channel_id=1, source_target_pairs={{0,2},{1,3},{2,0},{3,1},{4,6},{5,7},{6,4},{7,5},{8,10},{9,11},{10,... | collective-permute-start | bytes 3145736 | tf_op jit(solution)/shard_map/ppermute | solution.py:18
  25.1 18.5 %copy-start.2 = (f32[2,256,256]{2,1,0:T(8,128)S(1)}, f32[2,256,256]{2,1,0:T(8,128)}, u32[]{:S(2)}) copy-start(f32[2,256,256]{2,1,0:T(8,128)} %weight.20) | copy-start | bytes 1572868
  28.3 1.0 copy-start.11
  29.3 18.2 %copy-start.1 = (f32[2,1024,256]{2,1,0:T(8,128)S(1)}, f32[2,1024,256]{2,1,0:T(8,128)}, u32[]{:S(2)}) copy-start(f32[2,1024,256]{2,1,0:T(8,128)} %adjoint.3) | copy-start | bytes 6291460
  46.5 1.0 copy-start.7
  47.5 18.6 %copy-start.13 = (f32[1024,256]{1,0:T(8,128)}, f32[1024,256]{1,0:T(8,128)S(1)}, u32[]{:S(2)}) copy-start(f32[1024,256]{1,0:T(8,128)S(1)} %get-tuple-element.40) | copy-start | bytes 3145732
  47.5 1.6 copy-start.8
  52.6 49.4 %collective-permute-start.8 = (f32[1024,256]{1,0:T(8,128)}, f32[1024,256]{1,0:T(8,128)}, u32[]{:S(2)}, u32[]{:S(2)}) collective-permute-start(f32[1024,256]{1,0:T(8,128)} %get-tuple-element.46), channel_id=1, source_target_pairs={{0,2},{1,3},{2,0},{3,1},{4,6},{5,7},{6,4},{7,5},{8,10},{9,11},{10,... | collective-permute-start | bytes 3145736 | tf_op jit(solution)/shard_map/ppermute | solution.py:18
  66.1 1.2 copy-start.12
  70.2 1.0 copy-start.9
  71.2 14.7 %copy-start.15 = (f32[1024,256]{1,0:T(8,128)}, f32[1024,256]{1,0:T(8,128)S(1)}, u32[]{:S(2)}) copy-start(f32[1024,256]{1,0:T(8,128)S(1)} %get-tuple-element.43) | copy-start | bytes 3145732
  71.2 1.6 copy-start.10
  81.1 6.0 %copy-start.17 = (f32[1024,256]{1,0:T(8,128)}, f32[1024,256]{1,0:T(8,128)S(1)}, u32[]{:S(2)}) copy-start(f32[1024,256]{1,0:T(8,128)S(1)} %get-tuple-element.49) | copy-start | bytes 3145732
  85.9 1.4 copy-start.19
  87.2 12.7 %collective-permute-start.16 = (f32[512,256]{1,0:T(8,128)}, f32[512,256]{1,0:T(8,128)}, u32[]{:S(2)}, u32[]{:S(2)}) collective-permute-start(f32[512,256]{1,0:T(8,128)} %bitcast.36), channel_id=1, source_target_pairs={{0,32},{32,0},{64,96},{96,64},{1,33},{33,1},{65,97},{97,65},{2,34}... | collective-permute-start | bytes 1572872 | tf_op jit(solution)/shard_map/ppermute | solution.py:18
  88.5 23.7 %collective-permute-start.10 = (f32[1024,256]{1,0:T(8,128)}, f32[1024,256]{1,0:T(8,128)}, u32[]{:S(2)}, u32[]{:S(2)}) collective-permute-start(f32[1024,256]{1,0:T(8,128)} %get-tuple-element.52), channel_id=1, source_target_pairs={{0,2},{1,3},{2,0},{3,1},{4,6},{5,7},{6,4},{7,5},{8,10},{9,11},{10,... | collective-permute-start | bytes 3145736 | tf_op jit(solution)/shard_map/ppermute | solution.py:18
  90.4 21.7 %copy-start.4 = (f32[1024,256]{1,0:T(8,128)S(1)}, f32[1024,256]{1,0:T(8,128)}, u32[]{:S(2)}) copy-start(f32[1024,256]{1,0:T(8,128)} %copy-done.3) | copy-start | bytes 3145732
  90.5 21.7 %copy-start.6 = (f32[1024,256]{1,0:T(8,128)S(1)}, f32[1024,256]{1,0:T(8,128)}, u32[]{:S(2)}) copy-start(f32[1024,256]{1,0:T(8,128)} %copy-done.5) | copy-start | bytes 3145732
  101.3 16.9 %collective-permute-start.17 = (f32[256,256]{1,0:T(8,128)S(1)}, f32[256,256]{1,0:T(8,128)S(1)}, u32[]{:S(2)}, u32[]{:S(2)}) collective-permute-start(f32[256,256]{1,0:T(8,128)S(1)} %slice_select_fusion), channel_id=1, source_target_pairs={{0,64},{32,96},{64,0},{96,32},{1,65},{33,97},{65,1},{97,33},{2,66}... | collective-permute-start | bytes 786440 | tf_op jit(solution)/shard_map/ppermute | solution.py:18
  112.2 20.0 %copy-start.18 = (f32[1024,256]{1,0:T(8,128)S(1)}, f32[1024,256]{1,0:T(8,128)}, u32[]{:S(2)}) copy-start(f32[1024,256]{1,0:T(8,128)} %copy-done.17) | copy-start | bytes 3145732
  112.2 20.0 %copy-start.20 = (f32[1024,256]{1,0:T(8,128)S(1)}, f32[1024,256]{1,0:T(8,128)}, u32[]{:S(2)}) copy-start(f32[1024,256]{1,0:T(8,128)} %copy-done.19) | copy-start | bytes 3145732
  112.2 22.4 %copy-start.14 = (f32[1024,256]{1,0:T(8,128)S(1)}, f32[1024,256]{1,0:T(8,128)}, u32[]{:S(2)}) copy-start(f32[1024,256]{1,0:T(8,128)} %copy-done.13) | copy-start | bytes 3145732
  112.2 22.4 %copy-start.16 = (f32[1024,256]{1,0:T(8,128)S(1)}, f32[1024,256]{1,0:T(8,128)}, u32[]{:S(2)}) copy-start(f32[1024,256]{1,0:T(8,128)} %copy-done.15) | copy-start | bytes 3145732
  117.3 9.3 %collective-permute-start.12 = (f32[256,256]{1,0:T(8,128)S(1)}, f32[256,256]{1,0:T(8,128)S(1)}, u32[]{:S(2)}, u32[]{:S(2)}) collective-permute-start(f32[256,256]{1,0:T(8,128)S(1)} %broadcast_select_fusion), channel_id=1, source_target_pairs={{0,32},{32,0},{64,96},{96,64},{1,33},{33,1},{65,97},{97,65},{2,34}... | collective-permute-start | bytes 786440 | tf_op jit(solution)/shard_map/ppermute | solution.py:18
  118.2 12.1 %collective-permute-start.18 = (f32[256,256]{1,0:T(8,128)S(1)}, f32[256,256]{1,0:T(8,128)S(1)}, u32[]{:S(2)}, u32[]{:S(2)}) collective-permute-start(f32[256,256]{1,0:T(8,128)S(1)} %select_add_fusion), channel_id=1, source_target_pairs={{0,64},{32,96},{64,0},{96,32},{1,65},{33,97},{65,1},{97,33},{2,66}... | collective-permute-start | bytes 786440 | tf_op jit(solution)/shard_map/ppermute | solution.py:18
  126.7 8.0 %collective-permute-start.13 = (f32[128,256]{1,0:T(8,128)S(1)}, f32[128,256]{1,0:T(8,128)S(1)}, u32[]{:S(2)}, u32[]{:S(2)}) collective-permute-start(f32[128,256]{1,0:T(8,128)S(1)} %slice_select_fusion.1), channel_id=1, source_target_pairs={{0,64},{32,96},{64,0},{96,32},{1,65},{33,97},{65,1},{97,33},{2,66}... | collective-permute-start | bytes 393224 | tf_op jit(solution)/shard_map/ppermute | solution.py:18
  130.3 13.8 %collective-permute-start.19 = (f32[512,256]{1,0:T(8,128)S(1)}, f32[512,256]{1,0:T(8,128)S(1)}, u32[]{:S(2)}, u32[]{:S(2)}) collective-permute-start(f32[512,256]{1,0:T(8,128)S(1)} %maximum_select_fusion.2), channel_id=1, source_target_pairs={{0,32},{32,0},{64,96},{96,64},{1,33},{33,1},{65,97},{97,65},{2,34}... | collective-permute-start | bytes 1572872 | tf_op jit(solution)/shard_map/ppermute | solution.py:18
  132.2 27.5 %collective-permute-start.6 = (f32[1024,256]{1,0:T(8,128)S(1)}, f32[1024,256]{1,0:T(8,128)S(1)}, u32[]{:S(2)}, u32[]{:S(2)}) collective-permute-start(f32[1024,256]{1,0:T(8,128)S(1)} %copy-done.18), channel_id=1, source_target_pairs={{0,1},{1,0},{2,3},{3,2},{4,5},{5,4},{6,7},{7,6},{8,9},{9,8},{10,11... | collective-permute-start | bytes 3145736 | tf_op jit(solution)/shard_map/ppermute | solution.py:18
  132.2 27.5 %collective-permute-start.7 = (f32[1024,256]{1,0:T(8,128)S(1)}, f32[1024,256]{1,0:T(8,128)S(1)}, u32[]{:S(2)}, u32[]{:S(2)}) collective-permute-start(f32[1024,256]{1,0:T(8,128)S(1)} %copy-done.20), channel_id=1, source_target_pairs={{0,1},{1,0},{2,3},{3,2},{4,5},{5,4},{6,7},{7,6},{8,9},{9,8},{10,11... | collective-permute-start | bytes 3145736 | tf_op jit(solution)/shard_map/ppermute | solution.py:18
  132.7 27.0 %collective-permute-start.9 = (f32[1024,256]{1,0:T(8,128)S(1)}, f32[1024,256]{1,0:T(8,128)S(1)}, u32[]{:S(2)}, u32[]{:S(2)}) collective-permute-start(f32[1024,256]{1,0:T(8,128)S(1)} %get-tuple-element.60), channel_id=1, source_target_pairs={{0,1},{1,0},{2,3},{3,2},{4,5},{5,4},{6,7},{7,6},{8,9},{9,8},{10,11... | collective-permute-start | bytes 3145736 | tf_op jit(solution)/shard_map/ppermute | solution.py:18
  134.6 25.1 %collective-permute-start.11 = (f32[1024,256]{1,0:T(8,128)S(1)}, f32[1024,256]{1,0:T(8,128)S(1)}, u32[]{:S(2)}, u32[]{:S(2)}) collective-permute-start(f32[1024,256]{1,0:T(8,128)S(1)} %get-tuple-element.64), channel_id=1, source_target_pairs={{0,1},{1,0},{2,3},{3,2},{4,5},{5,4},{6,7},{7,6},{8,9},{9,8},{10,11... | collective-permute-start | bytes 3145736 | tf_op jit(solution)/shard_map/ppermute | solution.py:18
  144.1 7.5 %collective-permute-start.14 = (f32[128,256]{1,0:T(8,128)S(1)}, f32[128,256]{1,0:T(8,128)S(1)}, u32[]{:S(2)}, u32[]{:S(2)}) collective-permute-start(f32[128,256]{1,0:T(8,128)S(1)} %select_add_fusion.2), channel_id=1, source_target_pairs={{0,64},{32,96},{64,0},{96,32},{1,65},{33,97},{65,1},{97,33},{2,66}... | collective-permute-start | bytes 393224 | tf_op jit(solution)/shard_map/ppermute | solution.py:18
  151.7 6.5 %collective-permute-start.15 = (f32[256,256]{1,0:T(8,128)S(1)}, f32[256,256]{1,0:T(8,128)S(1)}, u32[]{:S(2)}, u32[]{:S(2)}) collective-permute-start(f32[256,256]{1,0:T(8,128)S(1)} %maximum_select_fusion.3), channel_id=1, source_target_pairs={{0,32},{32,0},{64,96},{96,64},{1,33},{33,1},{65,97},{97,65},{2,34}... | collective-permute-start | bytes 786440 | tf_op jit(solution)/shard_map/ppermute | solution.py:18

commit v4 on v3

--- a/solution.py
+++ b/solution.py
@@ -192,6 +192,32 @@
     return flat.reshape(x.shape)
 
 
+def shift_from(value, axis, shift):
+    n = lax.axis_size(axis)
+    return lax.ppermute(value, axis, [(source, (source + shift) % n) for source in range(n)])
+
+
+def batch_sum_wide(x, axis):
+    n = lax.axis_size(axis)
+    me = lax.axis_index(axis)
+    flat = x.reshape(n, -1, x.shape[-1])
+    shifts = range(1, n)
+    got = [shift_from(lax.dynamic_index_in_dim(flat, (me + k) % n, 0, keepdims=False), axis, k) for k in shifts]
+    total = lax.dynamic_index_in_dim(flat, me, 0, keepdims=False)
+    for g in got:
+        total = total + g
+    back = [shift_from(total, axis, k) for k in shifts]
+    pieces = [total] + back
+    rows = []
+    for j in range(n):
+        owner = (me - j) % n
+        piece = pieces[0]
+        for k in shifts:
+            piece = jnp.where(owner == k, pieces[k], piece)
+        rows.append(piece)
+    return jnp.stack(rows).reshape(x.shape)
+
+
 def local(leaves, leaf_order, node_order, weight_one, weight_two, top_adjoint):
     here = lax.axis_index("region")
     across = jnp.bitwise_xor(here, jnp.int32(1))
@@ -248,7 +274,7 @@
     early = batch_sum(jnp.stack(counts_two + [counts_one[s] for s in range(second, first)]), "batch")
     grad_two = early[:second]
     early = (grad_two, early[second:])
-    late = batch_sum(jnp.stack([counts_one[s] for s in range(second)]), "batch")
+    late = batch_sum_wide(jnp.stack([counts_one[s] for s in range(second)]), "batch")
     grad_one = place_grads(table, late, early[1])
     return (jnp.stack(top_log), leaf_adjoint, grad_one, grad_two)
 

time: 163 us -> 161 us (0.988)
  the two profiles are of different devices: /device:TPU:16 before, /device:TPU:1 now
where the time goes in v4:
time: 161 us; the launch traced here: 160 us
  Pallas kernels  59.7 us (37%)
  waiting for transfers between devices  47 us (29%)
  starting transfers between devices  33.4 us (21%)
  local copies, waits for them, and re-layouts  12.5 us (8%)
  other arithmetic  6.38 us (4%)
    pallas_call x18, Pallas kernels, call(): pl.pallas_call(kernel, grid_spec=pltpu.PrefetchScalarGridSpec(num_scalar_...  59.7 us
    ppermute x16, waiting for transfers between devices, from_partner(): return lax.ppermute(value, axis, pairs)  43.5 us
    ppermute x16, starting transfers between devices, from_partner(): return lax.ppermute(value, axis, pairs)  27.9 us
    unnamed x42, local copies, waits for them, and re-layouts  11.5 us
    ppermute x6, starting transfers between devices, shift_from(): lax.ppermute(value, axis, [(source, (source + shift) % n) for source in r...  5.58 us
    ppermute x6, waiting for transfers between devices, shift_from(): lax.ppermute(value, axis, [(source, (source + shift) % n) for source in r...  3.45 us
  transfers between devices with their start and end apart: 22, of which 7 were waited for; matrix products, arithmetic and copies ran while one was open for 3% of the time, Pallas kernels for 35%

profile of v4, /device:TPU:1, one launch (start us, length us, event | category | flops | bytes accessed | tf_op | source)
XLA Modules:
  0.0 160.1 jit_solution(5533918849247375225)
XLA Ops:
  2.8 1.8 %shard_map.95 = f32[1024,256]{1,0:T(8,128)S(1)} custom-call(s32[12]{0:T(128)S(1)} %pad_add_fusion.1.table, f32[8,1024,256]{2,1,0:T(8,128)} %left.7), custom_call_target="tpu_custom_call" | custom-call | bytes 2097152 | tf_op jit(solution)/shard_map/pallas_call | solution.py:40
  4.7 1.5 collective-permute-start.1
  6.1 1.8 %shard_map.100 = f32[1024,256]{1,0:T(8,128)S(1)} custom-call(s32[12]{0:T(128)S(1)} %pad_add_fusion.1.table, f32[8,1024,256]{2,1,0:T(8,128)} %left.7), custom_call_target="tpu_custom_call" | custom-call | bytes 2097152 | tf_op jit(solution)/shard_map/pallas_call | solution.py:40
  8.1 2.8 %shard_map.98 = f32[1024,256]{1,0:T(8,128)} custom-call(s32[12]{0:T(128)S(1)} %pad_add_fusion.1.table, f32[8,1024,256]{2,1,0:T(8,128)} %left.7), custom_call_target="tpu_custom_call" | custom-call | bytes 2097152 | tf_op jit(solution)/shard_map/pallas_call | solution.py:40
  11.4 2.8 %shard_map.93 = f32[1024,256]{1,0:T(8,128)} custom-call(s32[12]{0:T(128)S(1)} %pad_add_fusion.1.table, f32[8,1024,256]{2,1,0:T(8,128)} %left.7), custom_call_target="tpu_custom_call" | custom-call | bytes 2097152 | tf_op jit(solution)/shard_map/pallas_call | solution.py:40
  14.2 3.9 %shard_map.96 = (f32[1024,256]{1,0:T(8,128)}, f32[1024,256]{1,0:T(8,128)S(1)}, f32[1024,256]{1,0:T(8,128)S(1)}) custom-call(s32[12]{0:T(128)S(1)} %pad_add_fusion.1.table, f32[8,1024,256]{2,1,0:T(8,128)} %left.7, f32[1,1024,256]{2,1,0:T(8,128)S(1)} %bitcast.86, f32[4,256,256]{2,1,0:T(8,128)S(1)} %copy-done), custom_call_target="tpu_custom_call" | custom-call | flops 134217728 | bytes 5505024 | tf_op jit(solution)/shard_map/pallas_call | solution.py:40
  18.1 1.8 %collective-permute-start.2 = (f32[1024,256]{1,0:T(8,128)}, f32[1024,256]{1,0:T(8,128)}, u32[]{:S(2)}, u32[]{:S(2)}) collective-permute-start(f32[1024,256]{1,0:T(8,128)} %get-tuple-element.39), channel_id=1, source_target_pairs={{0,2},{1,3},{2,0},{3,1},{4,6},{5,7},{6,4},{7,5},{8,10},{9,11},{10,... | collective-permute-start | bytes 3145736 | tf_op jit(solution)/shard_map/ppermute | solution.py:18
  19.8 3.9 %shard_map.101 = (f32[1024,256]{1,0:T(8,128)}, f32[1024,256]{1,0:T(8,128)S(1)}, f32[1024,256]{1,0:T(8,128)S(1)}) custom-call(s32[12]{0:T(128)S(1)} %pad_add_fusion.1.table, f32[8,1024,256]{2,1,0:T(8,128)} %left.7, f32[1,1024,256]{2,1,0:T(8,128)S(1)} %bitcast.85, f32[4,256,256]{2,1,0:T(8,128)S(1)} %copy-done), custom_call_target="tpu_custom_call" | custom-call | flops 134217728 | bytes 5505024 | tf_op jit(solution)/shard_map/pallas_call | solution.py:40
  23.7 1.0 copy-done.3
  24.7 1.0 copy-done.5
  25.7 3.2 %shard_map.99 = (f32[1024,256]{1,0:T(8,128)S(1)}, f32[1024,256]{1,0:T(8,128)S(1)}, f32[1024,256]{1,0:T(8,128)S(1)}) custom-call(s32[12]{0:T(128)S(1)} %pad_add_fusion.1.table, f32[8,1024,256]{2,1,0:T(8,128)} %left.7, f32[1,1024,256]{2,1,0:T(8,128)} %bitcast.5.right, f32[4,256,256]{2,1,0:T(8,128)S(1)} %copy-done), custom_call_target="tpu_custom_call" | custom-call | flops 134217728 | bytes 5505024 | tf_op jit(solution)/shard_map/pallas_call | solution.py:40
  29.9 3.3 %shard_map.94 = (f32[1024,256]{1,0:T(8,128)S(1)}, f32[1024,256]{1,0:T(8,128)S(1)}, f32[1024,256]{1,0:T(8,128)S(1)}) custom-call(s32[12]{0:T(128)S(1)} %pad_add_fusion.1.table, f32[8,1024,256]{2,1,0:T(8,128)} %left.7, f32[1,1024,256]{2,1,0:T(8,128)} %bitcast.right, f32[4,256,256]{2,1,0:T(8,128)S(1)} %copy-done), custom_call_target="tpu_custom_call" | custom-call | flops 134217728 | bytes 5505024 | tf_op jit(solution)/shard_map/pallas_call | solution.py:40
  33.2 10.0 %collective-permute-done.2 = f32[1024,256]{1,0:T(8,128)} collective-permute-done((f32[1024,256]{1,0:T(8,128)}, f32[1024,256]{1,0:T(8,128)}, u32[]{:S(2)}, u32[]{:S(2)}) %collective-permute-start.2) | collective-permute-done | bytes 1048608 | tf_op jit(solution)/shard_map/ppermute | solution.py:18
  43.2 2.9 %shard_map.97 = (f32[1024,256]{1,0:T(8,128)S(1)}, f32[1024,256]{1,0:T(8,128)S(1)}, f32[1024,256]{1,0:T(8,128)S(1)}) custom-call(s32[12]{0:T(128)S(1)} %pad_add_fusion.1.table, f32[1,1024,256]{2,1,0:T(8,128)S(1)} %bitcast.82, f32[1,1024,256]{2,1,0:T(8,128)} %bitcast.3.right, f32[2,256,256]{2,1,0:T(8,128)S(1)} %copy-done.2), custom_call_target="tpu_custom_call" | custom-call | flops 134217728 | bytes 5505024 | tf_op jit(solution)/shard_map/pallas_call | solution.py:40
  47.1 1.6 %copy-done.8 = f32[1024,256]{1,0:T(8,128)S(1)} copy-done((f32[1024,256]{1,0:T(8,128)S(1)}, f32[1024,256]{1,0:T(8,128)}, u32[]{:S(2)}) %copy-start.8) | copy-done | bytes 1048600
  48.7 3.5 %shard_map.103 = (f32[256,256]{1,0:T(8,128)S(1)}, f32[1024,256]{1,0:T(8,128)}) custom-call(s32[12]{0:T(128)S(1)} %pad_add_fusion.1.table, f32[2,1024,256]{2,1,0:T(8,128)S(1)} %copy-done.1, f32[1,1024,256]{2,1,0:T(8,128)S(1)} %bitcast.77, f32[1,1024,256]{2,1,0:T(8,128)S(1)} %bitcast.78, f32[2,256,256]{2,1,0:T(8,128)S(1)} %copy-done.2), custom_call_target="tpu_custom_call" | custom-call | flops 268435456 | bytes 5767168 | tf_op jit(solution)/shard_map/pallas_call | solution.py:40
  52.3 1.2 collective-permute-start.8
  53.4 12.2 %collective-permute-done.5 = f32[1024,256]{1,0:T(8,128)} collective-permute-done((f32[1024,256]{1,0:T(8,128)}, f32[1024,256]{1,0:T(8,128)}, u32[]{:S(2)}, u32[]{:S(2)}) %collective-permute-start.5) | collective-permute-done | bytes 1048608 | tf_op jit(solution)/shard_map/ppermute | solution.py:18
  65.7 1.2 copy-done.12
  66.9 2.9 %shard_map.102 = (f32[1024,256]{1,0:T(8,128)S(1)}, f32[1024,256]{1,0:T(8,128)S(1)}, f32[1024,256]{1,0:T(8,128)S(1)}) custom-call(s32[12]{0:T(128)S(1)} %pad_add_fusion.1.table, f32[1,1024,256]{2,1,0:T(8,128)S(1)} %bitcast.81, f32[1,1024,256]{2,1,0:T(8,128)} %bitcast.8.right, f32[2,256,256]{2,1,0:T(8,128)S(1)} %copy-done.2), custom_call_target="tpu_custom_call" | custom-call | flops 134217728 | bytes 5505024 | tf_op jit(solution)/shard_map/pallas_call | solution.py:40
  69.8 1.0 copy-done.9
  70.8 1.6 %copy-done.10 = f32[1024,256]{1,0:T(8,128)S(1)} copy-done((f32[1024,256]{1,0:T(8,128)S(1)}, f32[1024,256]{1,0:T(8,128)}, u32[]{:S(2)}) %copy-start.10) | copy-done | bytes 1048600
  72.4 3.5 %shard_map.105 = (f32[256,256]{1,0:T(8,128)S(1)}, f32[1024,256]{1,0:T(8,128)}) custom-call(s32[12]{0:T(128)S(1)} %pad_add_fusion.1.table, f32[2,1024,256]{2,1,0:T(8,128)S(1)} %copy-done.1, f32[1,1024,256]{2,1,0:T(8,128)S(1)} %bitcast.79, f32[1,1024,256]{2,1,0:T(8,128)S(1)} %bitcast.80, f32[2,256,256]{2,1,0:T(8,128)S(1)} %copy-done.2), custom_call_target="tpu_custom_call" | custom-call | flops 268435456 | bytes 5767168 | tf_op jit(solution)/shard_map/pallas_call | solution.py:40
  76.0 4.8 %shard_map.104 = (f32[256,256]{1,0:T(8,128)S(1)}, f32[1024,256]{1,0:T(8,128)S(1)}, f32[8,1024,256]{2,1,0:T(8,128)}) custom-call(s32[12]{0:T(128)S(1)} %pad_add_fusion.1.table, f32[1,1024,256]{2,1,0:T(8,128)} %bitcast.12.adjoint, f32[1,1024,256]{2,1,0:T(8,128)S(1)} %bitcast.75, f32[1,1024,256]{2,1,0:T(8,128)S(1)} %bitcast.76, f32[4,256,256]{2,1,0:T(8,128)S(1)} %copy-done), custom_call_target="tpu_custom_call" | custom-call | flops 268435456 | bytes 5767168 | tf_op jit(solution)/shard_map/pallas_call | solution.py:40
  80.7 4.8 %shard_map.106 = (f32[256,256]{1,0:T(8,128)S(1)}, f32[1024,256]{1,0:T(8,128)S(1)}, f32[8,1024,256]{2,1,0:T(8,128)}) custom-call(s32[12]{0:T(128)S(1)} %pad_add_fusion.1.table, f32[1,1024,256]{2,1,0:T(8,128)} %bitcast.18.adjoint, f32[1,1024,256]{2,1,0:T(8,128)S(1)} %bitcast.73, f32[1,1024,256]{2,1,0:T(8,128)S(1)} %bitcast.74, ...), custom_call_target="tpu_custom_call", output_to_operand_aliasing={{2}: (5, {})} | custom-call | flops 268435456 | bytes 5767168 | tf_op jit(solution)/shard_map/pallas_call | solution.py:40
  85.5 1.2 fusion.1
  86.9 1.2 collective-permute-start.18
  88.1 1.3 collective-permute-start.10
  89.4 9.6 %collective-permute-done.18 = f32[512,256]{1,0:T(8,128)} collective-permute-done((f32[512,256]{1,0:T(8,128)}, f32[512,256]{1,0:T(8,128)}, u32[]{:S(2)}, u32[]{:S(2)}) %collective-permute-start.18) | collective-permute-done | bytes 524320 | tf_op jit(solution)/shard_map/ppermute | solution.py:18
  99.0 1.3 bitcast_add_fusion
  100.3 2.9 %collective-permute-start.19 = (f32[256,256]{1,0:T(8,128)S(1)}, f32[256,256]{1,0:T(8,128)S(1)}, u32[]{:S(2)}, u32[]{:S(2)}) collective-permute-start(f32[256,256]{1,0:T(8,128)S(1)} %slice_select_fusion), channel_id=1, source_target_pairs={{0,64},{32,96},{64,0},{96,32},{1,65},{33,97},{65,1},{97,33},{2,66}... | collective-permute-start | bytes 786440 | tf_op jit(solution)/shard_map/ppermute | solution.py:18
  103.2 4.8 %shard_map.107 = (f32[256,256]{1,0:T(8,128)S(1)}, f32[1024,256]{1,0:T(8,128)S(1)}, f32[8,1024,256]{2,1,0:T(8,128)}) custom-call(s32[12]{0:T(128)S(1)} %pad_add_fusion.1.table, f32[1,1024,256]{2,1,0:T(8,128)} %bitcast.22.adjoint, f32[1,1024,256]{2,1,0:T(8,128)S(1)} %bitcast.65, f32[1,1024,256]{2,1,0:T(8,128)S(1)} %bitcast.66, ...), custom_call_target="tpu_custom_call", output_to_operand_aliasing={{2}: (5, {})} | custom-call | flops 268435456 | bytes 5767168 | tf_op jit(solution)/shard_map/pallas_call | solution.py:40
  107.9 1.0 copy-done.19
  108.9 2.0 %collective-permute-done.10 = f32[1024,256]{1,0:T(8,128)} collective-permute-done((f32[1024,256]{1,0:T(8,128)}, f32[1024,256]{1,0:T(8,128)}, u32[]{:S(2)}, u32[]{:S(2)}) %collective-permute-start.10) | collective-permute-done | bytes 1048608 | tf_op jit(solution)/shard_map/ppermute | solution.py:18
  110.9 4.8 %shard_map.108 = (f32[256,256]{1,0:T(8,128)S(1)}, f32[1024,256]{1,0:T(8,128)S(1)}, f32[8,1024,256]{2,1,0:T(8,128)}) custom-call(s32[12]{0:T(128)S(1)} %pad_add_fusion.1.table, f32[1,1024,256]{2,1,0:T(8,128)} %bitcast.26.adjoint, f32[1,1024,256]{2,1,0:T(8,128)S(1)} %bitcast.67, f32[1,1024,256]{2,1,0:T(8,128)S(1)} %bitcast.68, ...), custom_call_target="tpu_custom_call", output_to_operand_aliasing={{2}: (5, {})} | custom-call | flops 268435456 | bytes 5767168 | tf_op jit(solution)/shard_map/pallas_call | solution.py:40
  116.8 2.0 %collective-permute-start.14 = (f32[128,256]{1,0:T(8,128)S(1)}, f32[128,256]{1,0:T(8,128)S(1)}, u32[]{:S(2)}, u32[]{:S(2)}) collective-permute-start(f32[128,256]{1,0:T(8,128)S(1)} %get-tuple-element.85), channel_id=1, source_target_pairs={{0,96},{32,0},{64,32},{96,64},{1,97},{33,1},{65,33},{97,65},{2,98}... | collective-permute-start | bytes 393224 | tf_op jit(solution)/shard_map/ppermute | solution.py:197
  120.4 1.6 %collective-permute-start.20 = (f32[256,256]{1,0:T(8,128)S(1)}, f32[256,256]{1,0:T(8,128)S(1)}, u32[]{:S(2)}, u32[]{:S(2)}) collective-permute-start(f32[256,256]{1,0:T(8,128)S(1)} %select_add_fusion), channel_id=1, source_target_pairs={{0,64},{32,96},{64,0},{96,32},{1,65},{33,97},{65,1},{97,33},{2,66}... | collective-permute-start | bytes 786440 | tf_op jit(solution)/shard_map/ppermute | solution.py:18
  122.1 2.1 %collective-permute-done.13 = f32[128,256]{1,0:T(8,128)S(1)} collective-permute-done((f32[128,256]{1,0:T(8,128)S(1)}, f32[128,256]{1,0:T(8,128)S(1)}, u32[]{:S(2)}, u32[]{:S(2)}) %collective-permute-start.13) | collective-permute-done | bytes 131104 | tf_op jit(solution)/shard_map/ppermute | solution.py:197
  124.2 1.3 collective-permute-done.12
  125.9 1.1 collective-permute-start.16
  127.6 10.3 %collective-permute-start.6 = (f32[1024,256]{1,0:T(8,128)}, f32[1024,256]{1,0:T(8,128)S(1)}, u32[]{:S(2)}, u32[]{:S(2)}) collective-permute-start(f32[1024,256]{1,0:T(8,128)} %copy-done.17), channel_id=1, source_target_pairs={{0,1},{1,0},{2,3},{3,2},{4,5},{5,4},{6,7},{7,6},{8,9},{9,8},{10,11... | collective-permute-start | bytes 3145736 | tf_op jit(solution)/shard_map/ppermute | solution.py:18
  137.9 2.2 %collective-permute-start.9 = (f32[1024,256]{1,0:T(8,128)}, f32[1024,256]{1,0:T(8,128)S(1)}, u32[]{:S(2)}, u32[]{:S(2)}) collective-permute-start(f32[1024,256]{1,0:T(8,128)} %copy-done.19), channel_id=1, source_target_pairs={{0,1},{1,0},{2,3},{3,2},{4,5},{5,4},{6,7},{7,6},{8,9},{9,8},{10,11... | collective-permute-start | bytes 3145736 | tf_op jit(solution)/shard_map/ppermute | solution.py:18
  140.1 1.6 %collective-permute-start.11 = (f32[1024,256]{1,0:T(8,128)}, f32[1024,256]{1,0:T(8,128)S(1)}, u32[]{:S(2)}, u32[]{:S(2)}) collective-permute-start(f32[1024,256]{1,0:T(8,128)} %copy-done.20), channel_id=1, source_target_pairs={{0,1},{1,0},{2,3},{3,2},{4,5},{5,4},{6,7},{7,6},{8,9},{9,8},{10,11... | collective-permute-start | bytes 3145736 | tf_op jit(solution)/shard_map/ppermute | solution.py:18
  141.8 1.7 %collective-permute-start.21 = (f32[512,256]{1,0:T(8,128)S(1)}, f32[512,256]{1,0:T(8,128)S(1)}, u32[]{:S(2)}, u32[]{:S(2)}) collective-permute-start(f32[512,256]{1,0:T(8,128)S(1)} %maximum_select_fusion.1), channel_id=1, source_target_pairs={{0,32},{32,0},{64,96},{96,64},{1,33},{33,1},{65,97},{97,65},{2,34}... | collective-permute-start | bytes 1572872 | tf_op jit(solution)/shard_map/ppermute | solution.py:18
  143.5 1.5 pad_maximum_fusion
  145.1 9.7 %collective-permute-done.21 = f32[512,256]{1,0:T(8,128)S(1)} collective-permute-done((f32[512,256]{1,0:T(8,128)S(1)}, f32[512,256]{1,0:T(8,128)S(1)}, u32[]{:S(2)}, u32[]{:S(2)}) %collective-permute-start.21) | collective-permute-done | bytes 524320 | tf_op jit(solution)/shard_map/ppermute | solution.py:18
  155.7 1.5 shard_map.110
  157.3 2.6 %shard_map.109 = f32[8,1024,256]{2,1,0:T(8,128)} custom-call(s32[12]{0:T(128)S(1)} %pad_add_fusion.1.table, f32[1,1024,256]{2,1,0:T(8,128)S(1)} %bitcast.69, f32[1,1024,256]{2,1,0:T(8,128)S(1)} %bitcast.70, f32[1,1024,256]{2,1,0:T(8,128)S(1)} %bitcast.71, f32[1,1024,256]{2,1,0:T(8,128)S(1)} %bitcast.72, ...), custom_call_target="tpu_custom_call", output_to_operand_aliasing={{}: (5, {})} | custom-call | bytes 8388608 | tf_op jit(solution)/shard_map/pallas_call | solution.py:40
  (78 shorter events, 9.7 us)
Async XLA Ops:
  4.7 9.5 %collective-permute-start.1 = (f32[1024,256]{1,0:T(8,128)S(1)}, f32[1024,256]{1,0:T(8,128)S(1)}, u32[]{:S(2)}, u32[]{:S(2)}) collective-permute-start(f32[1024,256]{1,0:T(8,128)S(1)} %shard_map.95), channel_id=1, source_target_pairs={{0,1},{1,0},{2,3},{3,2},{4,5},{5,4},{6,7},{7,6},{8,9},{9,8},{10,11... | collective-permute-start | bytes 3145736 | tf_op jit(solution)/shard_map/ppermute | solution.py:18
  8.0 6.2 %copy-start = (f32[4,256,256]{2,1,0:T(8,128)S(1)}, f32[4,256,256]{2,1,0:T(8,128)}, u32[]{:S(2)}) copy-start(f32[4,256,256]{2,1,0:T(8,128)} %weight.23) | copy-start | bytes 3145732
  8.0 11.9 %collective-permute-start.4 = (f32[1024,256]{1,0:T(8,128)S(1)}, f32[1024,256]{1,0:T(8,128)S(1)}, u32[]{:S(2)}, u32[]{:S(2)}) collective-permute-start(f32[1024,256]{1,0:T(8,128)S(1)} %shard_map.100), channel_id=1, source_target_pairs={{0,1},{1,0},{2,3},{3,2},{4,5},{5,4},{6,7},{7,6},{8,9},{9,8},{10,11... | collective-permute-start | bytes 3145736 | tf_op jit(solution)/shard_map/ppermute | solution.py:18
  10.9 14.9 %collective-permute-start.3 = (f32[1024,256]{1,0:T(8,128)}, f32[1024,256]{1,0:T(8,128)}, u32[]{:S(2)}, u32[]{:S(2)}) collective-permute-start(f32[1024,256]{1,0:T(8,128)} %shard_map.98), channel_id=1, source_target_pairs={{0,1},{1,0},{2,3},{3,2},{4,5},{5,4},{6,7},{7,6},{8,9},{9,8},{10,11... | collective-permute-start | bytes 3145736 | tf_op jit(solution)/shard_map/ppermute | solution.py:18
  14.2 15.7 %collective-permute-start = (f32[1024,256]{1,0:T(8,128)}, f32[1024,256]{1,0:T(8,128)}, u32[]{:S(2)}, u32[]{:S(2)}) collective-permute-start(f32[1024,256]{1,0:T(8,128)} %shard_map.93), channel_id=1, source_target_pairs={{0,1},{1,0},{2,3},{3,2},{4,5},{5,4},{6,7},{7,6},{8,9},{9,8},{10,11... | collective-permute-start | bytes 3145736 | tf_op jit(solution)/shard_map/ppermute | solution.py:18
  18.1 25.1 %collective-permute-start.2 = (f32[1024,256]{1,0:T(8,128)}, f32[1024,256]{1,0:T(8,128)}, u32[]{:S(2)}, u32[]{:S(2)}) collective-permute-start(f32[1024,256]{1,0:T(8,128)} %get-tuple-element.39), channel_id=1, source_target_pairs={{0,2},{1,3},{2,0},{3,1},{4,6},{5,7},{6,4},{7,5},{8,10},{9,11},{10,... | collective-permute-start | bytes 3145736 | tf_op jit(solution)/shard_map/ppermute | solution.py:18
  23.7 1.0 copy-start.3
  24.7 1.0 copy-start.5
  25.7 39.9 %collective-permute-start.5 = (f32[1024,256]{1,0:T(8,128)}, f32[1024,256]{1,0:T(8,128)}, u32[]{:S(2)}, u32[]{:S(2)}) collective-permute-start(f32[1024,256]{1,0:T(8,128)} %get-tuple-element.42), channel_id=1, source_target_pairs={{0,2},{1,3},{2,0},{3,1},{4,6},{5,7},{6,4},{7,5},{8,10},{9,11},{10,... | collective-permute-start | bytes 3145736 | tf_op jit(solution)/shard_map/ppermute | solution.py:18
  25.7 17.5 %copy-start.2 = (f32[2,256,256]{2,1,0:T(8,128)S(1)}, f32[2,256,256]{2,1,0:T(8,128)}, u32[]{:S(2)}) copy-start(f32[2,256,256]{2,1,0:T(8,128)} %weight.20) | copy-start | bytes 1572868
  29.0 1.0 copy-start.11
  29.9 17.2 %copy-start.1 = (f32[2,1024,256]{2,1,0:T(8,128)S(1)}, f32[2,1024,256]{2,1,0:T(8,128)}, u32[]{:S(2)}) copy-start(f32[2,1024,256]{2,1,0:T(8,128)} %adjoint.3) | copy-start | bytes 6291460
  46.1 1.0 copy-start.7
  47.1 18.6 %copy-start.13 = (f32[1024,256]{1,0:T(8,128)}, f32[1024,256]{1,0:T(8,128)S(1)}, u32[]{:S(2)}) copy-start(f32[1024,256]{1,0:T(8,128)S(1)} %get-tuple-element.40) | copy-start | bytes 3145732
  47.1 1.6 %copy-start.8 = (f32[1024,256]{1,0:T(8,128)S(1)}, f32[1024,256]{1,0:T(8,128)}, u32[]{:S(2)}) copy-start(f32[1024,256]{1,0:T(8,128)} %copy-done.7) | copy-start | bytes 3145732
  52.3 50.9 %collective-permute-start.8 = (f32[1024,256]{1,0:T(8,128)}, f32[1024,256]{1,0:T(8,128)}, u32[]{:S(2)}, u32[]{:S(2)}) collective-permute-start(f32[1024,256]{1,0:T(8,128)} %get-tuple-element.46), channel_id=1, source_target_pairs={{0,2},{1,3},{2,0},{3,1},{4,6},{5,7},{6,4},{7,5},{8,10},{9,11},{10,... | collective-permute-start | bytes 3145736 | tf_op jit(solution)/shard_map/ppermute | solution.py:18
  65.7 1.2 copy-start.12
  69.8 1.0 copy-start.9
  70.8 14.7 %copy-start.15 = (f32[1024,256]{1,0:T(8,128)}, f32[1024,256]{1,0:T(8,128)S(1)}, u32[]{:S(2)}) copy-start(f32[1024,256]{1,0:T(8,128)S(1)} %get-tuple-element.43) | copy-start | bytes 3145732
  70.8 1.6 %copy-start.10 = (f32[1024,256]{1,0:T(8,128)S(1)}, f32[1024,256]{1,0:T(8,128)}, u32[]{:S(2)}) copy-start(f32[1024,256]{1,0:T(8,128)} %copy-done.9) | copy-start | bytes 3145732
  80.7 6.0 %copy-start.17 = (f32[1024,256]{1,0:T(8,128)}, f32[1024,256]{1,0:T(8,128)S(1)}, u32[]{:S(2)}) copy-start(f32[1024,256]{1,0:T(8,128)S(1)} %get-tuple-element.49) | copy-start | bytes 3145732
  85.5 1.4 copy-start.18
  86.9 12.1 %collective-permute-start.18 = (f32[512,256]{1,0:T(8,128)}, f32[512,256]{1,0:T(8,128)}, u32[]{:S(2)}, u32[]{:S(2)}) collective-permute-start(f32[512,256]{1,0:T(8,128)} %bitcast.47), channel_id=1, source_target_pairs={{0,32},{32,0},{64,96},{96,64},{1,33},{33,1},{65,97},{97,65},{2,34}... | collective-permute-start | bytes 1572872 | tf_op jit(solution)/shard_map/ppermute | solution.py:18
  88.1 22.8 %collective-permute-start.10 = (f32[1024,256]{1,0:T(8,128)}, f32[1024,256]{1,0:T(8,128)}, u32[]{:S(2)}, u32[]{:S(2)}) collective-permute-start(f32[1024,256]{1,0:T(8,128)} %get-tuple-element.52), channel_id=1, source_target_pairs={{0,2},{1,3},{2,0},{3,1},{4,6},{5,7},{6,4},{7,5},{8,10},{9,11},{10,... | collective-permute-start | bytes 3145736 | tf_op jit(solution)/shard_map/ppermute | solution.py:18
  89.4 21.5 %copy-start.4 = (f32[1024,256]{1,0:T(8,128)S(1)}, f32[1024,256]{1,0:T(8,128)}, u32[]{:S(2)}) copy-start(f32[1024,256]{1,0:T(8,128)} %copy-done.3) | copy-start | bytes 3145732
  89.4 21.5 %copy-start.6 = (f32[1024,256]{1,0:T(8,128)S(1)}, f32[1024,256]{1,0:T(8,128)}, u32[]{:S(2)}) copy-start(f32[1024,256]{1,0:T(8,128)} %copy-done.5) | copy-start | bytes 3145732
  100.3 20.1 %collective-permute-start.19 = (f32[256,256]{1,0:T(8,128)S(1)}, f32[256,256]{1,0:T(8,128)S(1)}, u32[]{:S(2)}, u32[]{:S(2)}) collective-permute-start(f32[256,256]{1,0:T(8,128)S(1)} %slice_select_fusion), channel_id=1, source_target_pairs={{0,64},{32,96},{64,0},{96,32},{1,65},{33,97},{65,1},{97,33},{2,66}... | collective-permute-start | bytes 786440 | tf_op jit(solution)/shard_map/ppermute | solution.py:18
  107.9 1.0 copy-start.19
  110.9 32.6 %copy-start.14 = (f32[1024,256]{1,0:T(8,128)S(1)}, f32[1024,256]{1,0:T(8,128)}, u32[]{:S(2)}) copy-start(f32[1024,256]{1,0:T(8,128)} %copy-done.13) | copy-start | bytes 3145732
  110.9 32.6 %copy-start.16 = (f32[1024,256]{1,0:T(8,128)S(1)}, f32[1024,256]{1,0:T(8,128)}, u32[]{:S(2)}) copy-start(f32[1024,256]{1,0:T(8,128)} %copy-done.15) | copy-start | bytes 3145732
  115.8 1.0 copy-start.20
  116.8 5.3 %collective-permute-start.14 = (f32[128,256]{1,0:T(8,128)S(1)}, f32[128,256]{1,0:T(8,128)S(1)}, u32[]{:S(2)}, u32[]{:S(2)}) collective-permute-start(f32[128,256]{1,0:T(8,128)S(1)} %get-tuple-element.85), channel_id=1, source_target_pairs={{0,96},{32,0},{64,32},{96,64},{1,97},{33,1},{65,33},{97,65},{2,98}... | collective-permute-start | bytes 393224 | tf_op jit(solution)/shard_map/ppermute | solution.py:197
  118.8 5.4 %collective-permute-start.13 = (f32[128,256]{1,0:T(8,128)S(1)}, f32[128,256]{1,0:T(8,128)S(1)}, u32[]{:S(2)}, u32[]{:S(2)}) collective-permute-start(f32[128,256]{1,0:T(8,128)S(1)} %get-tuple-element.86), channel_id=1, source_target_pairs={{0,64},{32,96},{64,0},{96,32},{1,65},{33,97},{65,1},{97,33},{2,66}... | collective-permute-start | bytes 393224 | tf_op jit(solution)/shard_map/ppermute | solution.py:197
  119.6 5.9 %collective-permute-start.12 = (f32[128,256]{1,0:T(8,128)S(1)}, f32[128,256]{1,0:T(8,128)S(1)}, u32[]{:S(2)}, u32[]{:S(2)}) collective-permute-start(f32[128,256]{1,0:T(8,128)S(1)} %get-tuple-element.84), channel_id=1, source_target_pairs={{0,32},{32,64},{64,96},{96,0},{1,33},{33,65},{65,97},{97,1},{2,34}... | collective-permute-start | bytes 393224 | tf_op jit(solution)/shard_map/ppermute | solution.py:197
  120.4 17.5 %collective-permute-start.20 = (f32[256,256]{1,0:T(8,128)S(1)}, f32[256,256]{1,0:T(8,128)S(1)}, u32[]{:S(2)}, u32[]{:S(2)}) collective-permute-start(f32[256,256]{1,0:T(8,128)S(1)} %select_add_fusion), channel_id=1, source_target_pairs={{0,64},{32,96},{64,0},{96,32},{1,65},{33,97},{65,1},{97,33},{2,66}... | collective-permute-start | bytes 786440 | tf_op jit(solution)/shard_map/ppermute | solution.py:18
  125.5 12.3 %collective-permute-start.15 = (f32[128,256]{1,0:T(8,128)S(1)}, f32[128,256]{1,0:T(8,128)S(1)}, u32[]{:S(2)}, u32[]{:S(2)}) collective-permute-start(f32[128,256]{1,0:T(8,128)S(1)} %fusion.3), channel_id=1, source_target_pairs={{0,96},{32,0},{64,32},{96,64},{1,97},{33,1},{65,33},{97,65},{2,98}... | collective-permute-start | bytes 393224 | tf_op jit(solution)/shard_map/ppermute | solution.py:197
  125.9 14.2 %collective-permute-start.16 = (f32[128,256]{1,0:T(8,128)S(1)}, f32[128,256]{1,0:T(8,128)S(1)}, u32[]{:S(2)}, u32[]{:S(2)}) collective-permute-start(f32[128,256]{1,0:T(8,128)S(1)} %fusion.3), channel_id=1, source_target_pairs={{0,64},{32,96},{64,0},{96,32},{1,65},{33,97},{65,1},{97,33},{2,66}... | collective-permute-start | bytes 393224 | tf_op jit(solution)/shard_map/ppermute | solution.py:197
  127.0 14.8 %collective-permute-start.17 = (f32[128,256]{1,0:T(8,128)S(1)}, f32[128,256]{1,0:T(8,128)S(1)}, u32[]{:S(2)}, u32[]{:S(2)}) collective-permute-start(f32[128,256]{1,0:T(8,128)S(1)} %fusion.3), channel_id=1, source_target_pairs={{0,32},{32,64},{64,96},{96,0},{1,33},{33,65},{65,97},{97,1},{2,34}... | collective-permute-start | bytes 393224 | tf_op jit(solution)/shard_map/ppermute | solution.py:197
  127.6 29.7 %collective-permute-start.6 = (f32[1024,256]{1,0:T(8,128)}, f32[1024,256]{1,0:T(8,128)S(1)}, u32[]{:S(2)}, u32[]{:S(2)}) collective-permute-start(f32[1024,256]{1,0:T(8,128)} %copy-done.17), channel_id=1, source_target_pairs={{0,1},{1,0},{2,3},{3,2},{4,5},{5,4},{6,7},{7,6},{8,9},{9,8},{10,11... | collective-permute-start | bytes 3145736 | tf_op jit(solution)/shard_map/ppermute | solution.py:18
  137.9 19.4 %collective-permute-start.7 = (f32[1024,256]{1,0:T(8,128)}, f32[1024,256]{1,0:T(8,128)S(1)}, u32[]{:S(2)}, u32[]{:S(2)}) collective-permute-start(f32[1024,256]{1,0:T(8,128)} %copy-done.18), channel_id=1, source_target_pairs={{0,1},{1,0},{2,3},{3,2},{4,5},{5,4},{6,7},{7,6},{8,9},{9,8},{10,11... | collective-permute-start | bytes 3145736 | tf_op jit(solution)/shard_map/ppermute | solution.py:18
  137.9 19.4 %collective-permute-start.9 = (f32[1024,256]{1,0:T(8,128)}, f32[1024,256]{1,0:T(8,128)S(1)}, u32[]{:S(2)}, u32[]{:S(2)}) collective-permute-start(f32[1024,256]{1,0:T(8,128)} %copy-done.19), channel_id=1, source_target_pairs={{0,1},{1,0},{2,3},{3,2},{4,5},{5,4},{6,7},{7,6},{8,9},{9,8},{10,11... | collective-permute-start | bytes 3145736 | tf_op jit(solution)/shard_map/ppermute | solution.py:18
  140.1 17.2 %collective-permute-start.11 = (f32[1024,256]{1,0:T(8,128)}, f32[1024,256]{1,0:T(8,128)S(1)}, u32[]{:S(2)}, u32[]{:S(2)}) collective-permute-start(f32[1024,256]{1,0:T(8,128)} %copy-done.20), channel_id=1, source_target_pairs={{0,1},{1,0},{2,3},{3,2},{4,5},{5,4},{6,7},{7,6},{8,9},{9,8},{10,11... | collective-permute-start | bytes 3145736 | tf_op jit(solution)/shard_map/ppermute | solution.py:18
  141.8 13.0 %collective-permute-start.21 = (f32[512,256]{1,0:T(8,128)S(1)}, f32[512,256]{1,0:T(8,128)S(1)}, u32[]{:S(2)}, u32[]{:S(2)}) collective-permute-start(f32[512,256]{1,0:T(8,128)S(1)} %maximum_select_fusion.1), channel_id=1, source_target_pairs={{0,32},{32,0},{64,96},{96,64},{1,33},{33,1},{65,97},{97,65},{2,34}... | collective-permute-start | bytes 1572872 | tf_op jit(solution)/shard_map/ppermute | solution.py:18
